TPU v7x, 256 devices: a whole 4x4x8 slice. The times are simulated.
256 devices in a mesh: row: 8 (over y, core), col: 32 (over x, z).
Axes of the slice: x: 4, y: 4, z: 8, core: 2. Of those that a mesh axis runs over, the one named last changes fastest.
Arguments:
- inputs: bfloat16 [1024, 8192], P('row', 'col'), may hold values from -6 to 6
- out_grad: bfloat16 [1024, 8192], P('row', 'col'), may hold values from -6 to 6
- in_weight: bfloat16 [8192, 3, 8192], P('col', None, 'row'), may hold values from -0.0625 to 0.0625
- out_weight: bfloat16 [8192, 8192], P('row', 'col'), may hold values from -0.0625 to 0.0625
- filter_taps: float32 [8192, 7], P('row'), may hold values from -2.4 to 2.4
Outputs:
- result: bfloat16 [1024, 8192], P('row', 'col')
- input_grad: bfloat16 [1024, 8192], P('row', 'col')
- in_grad: bfloat16 [8192, 3, 8192], P('col', None, 'row')
- out_w_grad: bfloat16 [8192, 8192], P('row', 'col')
- filter_grad: float32 [8192, 7], P(('row', 'col'))
All inputs are finite; a program needn't handle non-finite values.
Results may differ from a plain program's by a relative error of at most 0.03.
Values may be sent and summed in bfloat16 or wider, within the bound.
No kernel may reach another device: no remote copies, remote signals or barrier semaphores. Data moves between devices by JAX's collectives and lax.ppermute only.
A program may use at most 64 MiB of HBM per device.

v0:
```python
import math

import jax
import jax.numpy as jnp
from jax import lax
from jax.sharding import PartitionSpec as P


def from_behind(value, axis, by):
    devices = lax.axis_size(axis)
    pairs = [(i, i + by) for i in range(devices) if 0 <= i + by < devices]
    return lax.ppermute(value, axis, pairs)


def rows_in(operand):
    return lax.all_gather(operand, "row", axis=0, tiled=True)


def spread(summand):
    return lax.psum_scatter(
        summand.astype(jnp.bfloat16), "col", scatter_dimension=0, tiled=True
    ).astype(jnp.float32)


def collect(operand):
    return lax.all_gather(operand, "col", axis=0, tiled=True)


def fold_rows(row_fn, num_rows):
    return lax.psum_scatter(
        row_fn(jnp.int32(0), num_rows * lax.axis_size("row")).astype(jnp.bfloat16),
        "row",
        scatter_dimension=0,
        tiled=True,
    ).astype(jnp.float32)


def neighbour(operand, offset_dev):
    return from_behind(operand, "col", offset_dev)


def on_device(inputs, out_grad, in_weight, out_weight, filter_taps):
    tok_rows = inputs.shape[0]
    col_width = inputs.shape[1]
    row_width = out_weight.shape[0]
    kernel_len = filter_taps.shape[1]
    conv_lag = kernel_len - 1
    weight_flat = in_weight.reshape(col_width, 3 * row_width)
    whole_in = rows_in(inputs)
    all_tokens = whole_in.shape[0]
    grad_scale = 1.0 / math.sqrt(all_tokens)
    in_term = jnp.dot(whole_in, weight_flat, preferred_element_type=jnp.float32).reshape(
        all_tokens, 3, row_width
    )
    mixed_qkv = spread(in_term).astype(jnp.bfloat16)
    query_part = mixed_qkv[:, 0].astype(jnp.float32)
    key_part = mixed_qkv[:, 1].astype(jnp.float32)
    value_part = mixed_qkv[:, 2].astype(jnp.float32)
    kv_product = key_part * value_part
    local_len, channel_width = kv_product.shape
    earlier = neighbour(kv_product[local_len - conv_lag :], 1)
    padded = jnp.concatenate([earlier, kv_product], 0)
    conv_out = jnp.zeros((local_len, channel_width), jnp.float32)
    for offset in range(kernel_len):
        conv_out = (
            conv_out
            + filter_taps[:, offset] * padded[conv_lag - offset : conv_lag - offset + local_len]
        )
    gated_out = (query_part * conv_out).astype(jnp.bfloat16)
    gated_all = collect(gated_out[:, None, :])[:, 0, :]

    def out_rows(begin_row, num_rows):
        return jnp.dot(gated_all, out_weight, preferred_element_type=jnp.float32)

    projected = fold_rows(out_rows, tok_rows)
    result = (inputs.astype(jnp.float32) + projected).astype(jnp.bfloat16)
    whole_grad = rows_in(out_grad)
    out_w_grad = (
        lax.dot_general(
            gated_all, whole_grad, (((0,), (0,)), ((), ())), preferred_element_type=jnp.float32
        )
        * grad_scale
    ).astype(jnp.bfloat16)
    dy_term = lax.dot_general(
        whole_grad, out_weight, (((1,), (1,)), ((), ())), preferred_element_type=jnp.float32
    )
    grad_gated = spread(dy_term[:, None, :])[:, 0, :]
    grad_query = grad_gated * conv_out
    grad_conv = grad_gated * query_part
    following = neighbour(grad_conv[:conv_lag], -1)
    padded_back = jnp.concatenate([grad_conv, following], 0)
    grad_product = jnp.zeros((local_len, channel_width), jnp.float32)
    tap_terms = []
    for offset in range(kernel_len):
        grad_product = (
            grad_product + filter_taps[:, offset] * padded_back[offset : offset + local_len]
        )
        tap_terms.append(
            jnp.sum(grad_conv * padded[conv_lag - offset : conv_lag - offset + local_len], axis=0)
        )
    tap_stack = jnp.stack(tap_terms, axis=1)
    filter_grad = lax.psum_scatter(tap_stack, "col", scatter_dimension=0, tiled=True) * grad_scale
    grad_mixed = jnp.stack(
        [grad_query, grad_product * value_part, grad_product * key_part], axis=1
    ).astype(jnp.bfloat16)
    grad_all = collect(grad_mixed)
    grad_flat = grad_all.reshape(all_tokens, 3 * row_width)
    in_grad = (
        (
            lax.dot_general(
                whole_in, grad_flat, (((0,), (0,)), ((), ())), preferred_element_type=jnp.float32
            )
            * grad_scale
        )
        .astype(jnp.bfloat16)
        .reshape(col_width, 3, row_width)
    )

    def back_rows(begin_row, num_rows):
        return lax.dot_general(
            grad_flat, weight_flat, (((1,), (1,)), ((), ())), preferred_element_type=jnp.float32
        )

    back_sum = fold_rows(back_rows, tok_rows)
    input_grad = (out_grad.astype(jnp.float32) + back_sum).astype(jnp.bfloat16)
    return (result, input_grad, in_grad, out_w_grad, filter_grad)


def solution(mesh):
    placed = (
        P("row", "col"),
        P("row", "col"),
        P("col", None, "row"),
        P("row", "col"),
        P("row", None),
    )
    return jax.shard_map(
        on_device,
        mesh=mesh,
        in_specs=placed,
        out_specs=(
            P("row", "col"),
            P("row", "col"),
            P("col", None, "row"),
            P("row", "col"),
            P(("row", "col"), None),
        ),
        check_vma=False,
    )
```

profile of v0, /device:TPU:2, one launch (start us, length us, event | category | flops | bytes accessed | tf_op | source)
XLA Modules:
  0.0 948.6 jit_solution(61222789038099263)
XLA Ops:
  7.2 0.0 copy-start
  7.2 0.0 reduce-scatter.8.cloned.1.call-start
  7.2 14.0 %all_gather.12 = bf16[1024,256]{1,0:T(8,128)(2,1)S(1)} all-gather(bf16[128,256]{1,0:T(8,128)(2,1)} %param.5), channel_id=1, replica_groups=mesh['row'=8,'col'=32] {'row'}, dimensions={0}, use_global_device_ids=true | all-gather | bytes 589824 | tf_op jit(solution)/shard_map/all_gather | solution.py:16
  21.2 1.7 copy.14
  22.9 4.5 convolution_convert_fusion
  27.4 0.0 copy-start.3
  27.4 0.0 reduce-scatter.8.cloned.1.call-update
  27.4 0.0 reduce-scatter.12.cloned.1.call-start
  27.5 0.8 copy-done.3
  28.2 13.1 %all_gather.14 = bf16[1024,256]{1,0:T(8,128)(2,1)S(1)} all-gather(bf16[128,256]{1,0:T(8,128)(2,1)S(1)} %copy-done.3), channel_id=1, replica_groups=mesh['row'=8,'col'=32] {'row'}, dimensions={0}, use_global_device_ids=true | all-gather | bytes 589824 | tf_op jit(solution)/shard_map/all_gather | solution.py:16
  41.3 0.0 copy-done
  41.3 2.1 convert_bitcast_fusion
  43.4 0.0 copy-start.4
  43.4 0.0 reduce-scatter.12.cloned.1.call-update
  43.5 0.0 all-gather.6.cloned.1.call-start
  43.5 212.8 %reduce-scatter.8.cloned.1.call-done = bf16[32,3,1024]{2,0,1:T(8,128)(2,1)} async-done(((bf16[1024,3,1024]{2,0,1:T(8,128)(2,1)}), bf16[32,3,1024]{2,0,1:T(8,128)(2,1)}) %reduce-scatter.8.cloned.1.call-update) | async-done | bytes 196624 | tf_op jit(solution)/shard_map/reduce_scatter | solution.py:20
  256.3 0.9 convert_multiply_fusion.1
  257.2 2.8 collective-permute-start
  260.0 217.0 %reduce-scatter.12.cloned.1.call-done = bf16[32,1,1024]{2,0,1:T(8,128)(2,1)} async-done(((bf16[1024,1,1024]{2,0,1:T(8,128)(2,1)}), bf16[32,1,1024]{2,0,1:T(8,128)(2,1)}) %reduce-scatter.12.cloned.1.call-update) | async-done | bytes 65552 | tf_op jit(solution)/shard_map/reduce_scatter | solution.py:20
  477.0 0.0 collective-permute-done
  477.0 1.1 multiply_reduce_fusion
  478.2 4.6 collective-permute-start.1
  482.8 0.0 copy-done.4
  482.8 1.5 collective-permute-done.1
  484.4 1.1 fusion.32
  485.5 1.5 fusion.31
  487.1 0.0 all-gather.6.cloned.1.call-update
  487.1 0.0 reduce-scatter.16.cloned.1.call-start
  487.1 0.1 stack.51
  487.2 1.0 copy.17
  488.2 0.0 reduce-scatter.16.cloned.1.call-update
  488.2 0.0 all-gather.4.cloned.1.call-start
  488.3 0.7 pad_maximum_fusion
  489.0 0.0 all-gather.4.cloned.1.call-update
  489.0 0.0 copy-start.1
  489.0 0.0 reduce-scatter.10.cloned.1.call-start
  489.1 74.2 %all-gather.6.cloned.1.call-done = bf16[1024,1024]{1,0:T(8,128)(2,1)} async-done(((bf16[32,1024]{1,0:T(8,128)(2,1)}), bf16[1024,1024]{1,0:T(8,128)(2,1)}) %all-gather.6.cloned.1.call-update) | async-done | bytes 2097168 | tf_op jit(solution)/shard_map/all_gather | solution.py:26
  563.2 3.1 convolution_convert_fusion.1
  566.3 0.0 reduce-scatter.10.cloned.1.call-update
  566.4 0.0 reduce-scatter.14.cloned.1.call-start
  566.4 215.1 %reduce-scatter.16.cloned.1.call-done = f32[32,7]{1,0:T(8,128)} async-done(((f32[1024,7]{1,0:T(8,128)}), f32[32,7]{1,0:T(8,128)}) %reduce-scatter.16.cloned.1.call-update) | async-done | bytes 912
  781.5 0.8 copy.18
  782.3 0.6 broadcast_multiply_fusion
  782.9 87.2 %all-gather.4.cloned.1.call-done = bf16[1024,3,1024]{2,0,1:T(8,128)(2,1)} async-done(((bf16[32,3,1024]{2,0,1:T(8,128)(2,1)}), bf16[1024,3,1024]{2,0,1:T(8,128)(2,1)}) %all-gather.4.cloned.1.call-update) | async-done | bytes 6291472 | tf_op jit(solution)/shard_map/all_gather | solution.py:26
  870.0 0.0 copy-done.1
  870.0 5.4 fusion.2
  875.5 0.0 reduce-scatter.14.cloned.1.call-update
  875.5 0.0 copy-start.2
  875.5 3.2 fusion.3
  878.7 26.4 %reduce-scatter.10.cloned.1.call-done = bf16[128,256]{1,0:T(8,128)(2,1)} async-done(((bf16[1024,256]{1,0:T(8,128)(2,1)}), bf16[128,256]{1,0:T(8,128)(2,1)}) %reduce-scatter.10.cloned.1.call-update) | async-done | bytes 65552 | tf_op jit(solution)/shard_map/reduce_scatter | solution.py:30
  905.0 0.0 copy-done.2
  905.0 1.5 add_convert_fusion.1
  906.5 8.7 copy.15
  915.2 4.6 fusion
  919.8 1.7 copy.16
  921.6 18.7 %reduce-scatter.14.cloned.1.call-done = bf16[128,256]{1,0:T(8,128)(2,1)} async-done(((bf16[1024,256]{1,0:T(8,128)(2,1)}), bf16[128,256]{1,0:T(8,128)(2,1)}) %reduce-scatter.14.cloned.1.call-update) | async-done | bytes 65552 | tf_op jit(solution)/shard_map/reduce_scatter | solution.py:30
  940.2 1.5 add_convert_fusion
  (3 shorter events, 0.0 us)
Async XLA Ops:
  7.2 34.2 %copy-start = (bf16[1024,256]{1,0:T(8,128)(2,1)S(1)}, bf16[1024,256]{1,0:T(8,128)(2,1)}, u32[]{:S(2)}) copy-start(bf16[1024,256]{1,0:T(8,128)(2,1)} %param.8) | copy-start | bytes 1572868
  7.2 249.2 %reduce-scatter.8.cloned.1.call-start = ((), (), s32[]{:S(2)}) async-start(), calls=%async_computation.5 | async-start | bytes 6488064 | tf_op jit(solution)/shard_map/reduce_scatter | solution.py:20
  27.4 0.8 copy-start.3
  27.4 449.6 %reduce-scatter.12.cloned.1.call-start = ((), (), s32[]{:S(2)}) async-start(), calls=%async_computation.7 | async-start | bytes 2162688 | tf_op jit(solution)/shard_map/reduce_scatter | solution.py:20
  43.4 439.4 %copy-start.4 = (f32[1024,7]{0,1:T(8,128)S(1)}, f32[1024,7]{0,1:T(8,128)}, u32[]{:S(2)}) copy-start(f32[1024,7]{0,1:T(8,128)} %param.9) | copy-start | bytes 86020
  43.5 519.8 %all-gather.6.cloned.1.call-start = ((), (), s32[]{:S(2)}) async-start(), calls=%async_computation.10 | async-start | bytes 2162688 | tf_op jit(solution)/shard_map/all_gather | solution.py:26
  257.2 219.8 %collective-permute-start = (f32[6,1024]{1,0:T(8,128)S(1)}, f32[6,1024]{1,0:T(8,128)S(1)}, u32[]{:S(2)}, u32[]{:S(2)}) collective-permute-start(f32[6,1024]{1,0:T(8,128)S(1)} %slice.112), channel_id=1, source_target_pairs={{0,1},{1,2},{2,3},{3,4},{4,5},{5,6},{6,7},{7,8},{8,9},{9,10},{10,1... | collective-permute-start | bytes 73736 | tf_op jit(solution)/shard_map/ppermute | solution.py:12
  478.2 6.2 collective-permute-start.1
  487.1 294.4 %reduce-scatter.16.cloned.1.call-start = ((), (), s32[]{:S(2)}) async-start(), calls=%async_computation.11 | async-start | bytes 540672
  488.2 381.8 %all-gather.4.cloned.1.call-start = ((), (), s32[]{:S(2)}) async-start(), calls=%async_computation.8 | async-start | bytes 6488064 | tf_op jit(solution)/shard_map/all_gather | solution.py:26
  489.0 381.0 %copy-start.1 = (bf16[256,3,1024]{2,0,1:T(8,128)(2,1)S(1)}, bf16[256,3,1024]{2,0,1:T(8,128)(2,1)}, u32[]{:S(2)}) copy-start(bf16[256,3,1024]{2,0,1:T(8,128)(2,1)} %param.7) | copy-start | bytes 4718596
  489.0 416.0 %reduce-scatter.10.cloned.1.call-start = ((), (), s32[]{:S(2)}) async-start(), calls=%async_computation.6 | async-start | bytes 589824 | tf_op jit(solution)/shard_map/reduce_scatter | solution.py:30
  566.4 373.9 %reduce-scatter.14.cloned.1.call-start = ((), (), s32[]{:S(2)}) async-start(), calls=%async_computation.9 | async-start | bytes 589824 | tf_op jit(solution)/shard_map/reduce_scatter | solution.py:30
  875.5 29.5 %copy-start.2 = (bf16[128,256]{1,0:T(8,128)(2,1)S(1)}, bf16[128,256]{1,0:T(8,128)(2,1)}, u32[]{:S(2)}) copy-start(bf16[128,256]{1,0:T(8,128)(2,1)} %param.5) | copy-start | bytes 196612
Sparse Core Ops, SparseCore 0:
  27.6 228.7 reduce-scatter.7
  260.2 216.8 reduce-scatter.11
  487.2 76.0 all-gather.5
  567.5 213.9 reduce-scatter.15
  783.9 86.0 all-gather.3
  873.0 32.0 reduce-scatter.9
  907.5 32.6 reduce-scatter.13
where the time goes:
time: 949 us
  waiting for transfers between devices  853 us (90%)
  blocking collectives  27.1 us (3%)
  matrix products  22.9 us (2%)
  local copies, waits for them, and re-layouts  14.8 us (2%)
  between operations  14.2 us (1%)
    reduce_scatter x2, waiting for transfers between devices, spread(): lax.psum_scatter(summand.astype(jnp.bfloat16), 'col', scatter_dimension=0...  430 us
    unnamed x8, waiting for transfers between devices  215 us
    all_gather x2, waiting for transfers between devices, collect(): return lax.all_gather(operand, 'col', axis=0, tiled=True)  161 us
    reduce_scatter x2, waiting for transfers between devices, fold_rows(): lax.psum_scatter(row_fn(jnp.int32(0), num_rows * lax.axis_size('row')).as...  45 us
    all_gather x2, blocking collectives, rows_in(): return lax.all_gather(operand, 'row', axis=0, tiled=True)  27.1 us
  transfers between devices with their start and end apart: 9, of which 8 were waited for; matrix products, arithmetic and copies ran while one was open for 4% of the time, Pallas kernels for 0%

commit v1 on v0

v1 whole, which is shorter than its diff:
```python
import math

import jax
import jax.numpy as jnp
from jax import lax
from jax.sharding import PartitionSpec as P


def rows_in(operand):
    return lax.all_gather(operand, "row", axis=0, tiled=True)


def fold_rows(summand):
    return lax.psum_scatter(
        summand.astype(jnp.bfloat16), "row", scatter_dimension=0, tiled=True
    ).astype(jnp.float32)


def sum_cols(summand):
    return lax.psum(summand.astype(jnp.bfloat16), "col")


def shifted(values, by):
    tokens = values.shape[0]
    if by == 0:
        return values
    pad = jnp.zeros((abs(by),) + values.shape[1:], values.dtype)
    if by > 0:
        return jnp.concatenate([pad, values[: tokens - by]], 0)
    return jnp.concatenate([values[-by:], pad], 0)


def on_device(inputs, out_grad, in_weight, out_weight, filter_taps):
    col_width = inputs.shape[1]
    row_width = out_weight.shape[0]
    kernel_len = filter_taps.shape[1]
    weight_flat = in_weight.reshape(col_width, 3 * row_width)
    whole_in = rows_in(inputs)
    all_tokens = whole_in.shape[0]
    grad_scale = 1.0 / math.sqrt(all_tokens)

    in_term = jnp.dot(whole_in, weight_flat, preferred_element_type=jnp.float32)
    mixed_qkv = sum_cols(in_term).reshape(all_tokens, 3, row_width)
    query_part = mixed_qkv[:, 0].astype(jnp.float32)
    key_part = mixed_qkv[:, 1].astype(jnp.float32)
    value_part = mixed_qkv[:, 2].astype(jnp.float32)
    kv_product = key_part * value_part
    conv_out = jnp.zeros_like(kv_product)
    for offset in range(kernel_len):
        conv_out = conv_out + filter_taps[:, offset] * shifted(kv_product, offset)
    gated_all = (query_part * conv_out).astype(jnp.bfloat16)

    projected = fold_rows(
        jnp.dot(gated_all, out_weight, preferred_element_type=jnp.float32)
    )
    result = (inputs.astype(jnp.float32) + projected).astype(jnp.bfloat16)

    whole_grad = rows_in(out_grad)
    out_w_grad = (
        lax.dot_general(
            gated_all, whole_grad, (((0,), (0,)), ((), ())), preferred_element_type=jnp.float32
        )
        * grad_scale
    ).astype(jnp.bfloat16)
    dy_term = lax.dot_general(
        whole_grad, out_weight, (((1,), (1,)), ((), ())), preferred_element_type=jnp.float32
    )
    grad_gated = sum_cols(dy_term).astype(jnp.float32)
    grad_query = grad_gated * conv_out
    grad_conv = grad_gated * query_part
    grad_product = jnp.zeros_like(grad_conv)
    tap_terms = []
    for offset in range(kernel_len):
        grad_product = grad_product + filter_taps[:, offset] * shifted(grad_conv, -offset)
        tap_terms.append(jnp.sum(grad_conv * shifted(kv_product, offset), axis=0))
    tap_stack = jnp.stack(tap_terms, axis=1)
    cols = lax.axis_size("col")
    own = row_width // cols
    filter_grad = (
        lax.dynamic_slice_in_dim(tap_stack, lax.axis_index("col") * own, own, 0) * grad_scale
    )
    grad_mixed = jnp.stack(
        [grad_query, grad_product * value_part, grad_product * key_part], axis=1
    ).astype(jnp.bfloat16)
    grad_flat = grad_mixed.reshape(all_tokens, 3 * row_width)
    in_grad = (
        (
            lax.dot_general(
                whole_in, grad_flat, (((0,), (0,)), ((), ())), preferred_element_type=jnp.float32
            )
            * grad_scale
        )
        .astype(jnp.bfloat16)
        .reshape(col_width, 3, row_width)
    )
    back_sum = fold_rows(
        lax.dot_general(
            grad_flat, weight_flat, (((1,), (1,)), ((), ())), preferred_element_type=jnp.float32
        )
    )
    input_grad = (out_grad.astype(jnp.float32) + back_sum).astype(jnp.bfloat16)
    return (result, input_grad, in_grad, out_w_grad, filter_grad)


def solution(mesh):
    placed = (
        P("row", "col"),
        P("row", "col"),
        P("col", None, "row"),
        P("row", "col"),
        P("row", None),
    )
    return jax.shard_map(
        on_device,
        mesh=mesh,
        in_specs=placed,
        out_specs=(
            P("row", "col"),
            P("row", "col"),
            P("col", None, "row"),
            P("row", "col"),
            P(("row", "col"), None),
        ),
        check_vma=False,
    )
```

time: 949 us -> 404 us (0.43)
  waiting for transfers between devices: 853 us -> 248 us
  local copies, waits for them, and re-layouts: 14.8 us -> 46.9 us
  other arithmetic: 8.99 us -> 40.8 us
    reduce_scatter x4 -> x2, waiting for transfers between devices: 475 us -> 34.4 us  [fold_rows(): lax.psum_scatter(summand.astype(jnp.bfloat16), 'row', scatter_dimension=0...]
    unnamed x8 -> x3, waiting for transfers between devices: 215 us -> 0.05 us
    psum x0 -> x1, waiting for transfers between devices: none -> 213 us  [sum_cols(): return lax.psum(summand.astype(jnp.bfloat16), 'col')]
    all_gather x2 -> x0, waiting for transfers between devices: 161 us -> none  [collect(): return lax.all_gather(operand, 'col', axis=0, tiled=True)]
    another operation x3 -> x2, other arithmetic: 3.39 us -> 23.1 us  [on_device(): jnp.stack([grad_query, grad_product * value_part, grad_product * key_part...]
    convert_element_type x0 -> x2, local copies, waits for them, and re-layouts: none -> 17.5 us  [the longest x1 8.83 us: on_device(): grad_mixed = jnp.stack([grad_query, grad_product * value_part, grad_produ...]
    slice x3 -> x7, local copies, waits for them, and re-layouts: 0.03 us -> 15.1 us  [the longest x6 15.1 us: shifted(): return jnp.concatenate([values[-by:], pad], 0)]
  transfers between devices with their start and end apart: 9 -> 3, of which waited for: 8 -> 3; matrix products, arithmetic and copies ran while one was open for 4% -> 8% of each run, Pallas kernels for 0% -> 0%
where the time goes in v1:
time: 404 us; the launch traced here: 403 us
  waiting for transfers between devices  248 us (61%)
  local copies, waits for them, and re-layouts  46.9 us (12%)
  other arithmetic  40.8 us (10%)
  blocking collectives  27.3 us (7%)
  matrix products  25.4 us (6%)
  between operations  13.8 us (3%)
    psum x1, waiting for transfers between devices, sum_cols(): return lax.psum(summand.astype(jnp.bfloat16), 'col')  213 us
    reduce_scatter x2, waiting for transfers between devices, fold_rows(): lax.psum_scatter(summand.astype(jnp.bfloat16), 'row', scatter_dimension=0...  34.4 us
    all_gather x2, blocking collectives, rows_in(): return lax.all_gather(operand, 'row', axis=0, tiled=True)  27.3 us
    another operation x2, other arithmetic, on_device(): jnp.stack([grad_query, grad_product * value_part, grad_product * key_part...  23.1 us
    slice x6, local copies, waits for them, and re-layouts, shifted(): return jnp.concatenate([values[-by:], pad], 0)  15.1 us
    convert_element_type x1, local copies, waits for them, and re-layouts, on_device(): grad_mixed = jnp.stack([grad_query, grad_product * value_part, grad_produ...  8.83 us
    reshape x1, local copies, waits for them, and re-layouts, on_device(): mixed_qkv = sum_cols(in_term).reshape(all_tokens, 3, row_width)  8.7 us
    convert_element_type x1, local copies, waits for them, and re-layouts, sum_cols(): return lax.psum(summand.astype(jnp.bfloat16), 'col')  8.67 us
  transfers between devices with their start and end apart: 3, of which 3 were waited for; matrix products, arithmetic and copies ran while one was open for 8% of the time, Pallas kernels for 0%

profile of v1, /device:TPU:2, one launch (start us, length us, event | category | flops | bytes accessed | tf_op | source)
XLA Modules:
  0.0 402.6 jit_solution(17833018171722416195)
XLA Ops:
  7.2 0.0 copy-start
  7.2 0.0 all-reduce.15.cloned.1.call-start
  7.2 14.0 %all_gather.6 = bf16[1024,256]{1,0:T(8,128)(2,1)S(1)} all-gather(bf16[128,256]{1,0:T(8,128)(2,1)} %param.5), channel_id=1, replica_groups=mesh['row'=8,'col'=32] {'row'}, dimensions={0}, use_global_device_ids=true | all-gather | bytes 589824 | tf_op jit(solution)/shard_map/all_gather | solution.py:10
  21.2 0.0 copy-start.6
  21.2 13.3 %all_gather.7 = bf16[1024,256]{1,0:T(8,128)(2,1)S(1)} all-gather(bf16[128,256]{1,0:T(8,128)(2,1)} %param.6), channel_id=1, replica_groups=mesh['row'=8,'col'=32] {'row'}, dimensions={0}, use_global_device_ids=true | all-gather | bytes 589824 | tf_op jit(solution)/shard_map/all_gather | solution.py:10
  34.5 0.0 copy-start.4
  34.5 1.9 copy.12
  36.4 4.5 %convolution_convert_fusion = bf16[1024,3072]{1,0:T(8,128)(2,1)} fusion(bf16[1024,256]{1,0:T(8,128)(2,1)S(1)} %all_gather.6, bf16[256,3072]{0,1:T(8,128)(2,1)S(1)} %bitcast.110), kind=kOutput, calls=%fused_computation.1 | convolution fusion | flops 1613758464 | bytes 8388608 | tf_op jit(solution)/shard_map/dot_general | solution.py:42
  40.9 0.0 copy-done.6
  40.9 8.7 %copy.13 = bf16[1024,3072]{0,1:T(8,128)(2,1)} copy(bf16[1024,3072]{1,0:T(8,128)(2,1)} %convolution_convert_fusion) | data formatting | bytes 12582912 | tf_op jit(solution)/shard_map/convert_element_type | solution.py:20
  49.6 8.7 %copy.14 = bf16[1024,3,1024]{2,0,1:T(8,128)(2,1)} copy(bf16[1024,3,1024]{0,2,1:T(8,128)(2,1)} %bitcast.108) | data formatting | bytes 12582912 | tf_op jit(solution)/shard_map/reshape | solution.py:43
  58.3 0.0 copy-done.4
  58.3 0.0 copy-done
  58.3 2.1 convolution_convert_fusion.1
  60.4 0.0 copy-start.11
  60.4 0.0 all-reduce.15.cloned.1.call-update
  60.4 0.2 reduce-scatter.3.cloned.1.call-start
  60.6 0.5 copy-done.11
  61.2 213.4 %all-reduce.15.cloned.1.call-done = (bf16[1024,3,1024]{2,0,1:T(8,128)(2,1)}, bf16[1024,1024]{1,0:T(8,128)(2,1)}) async-done(((bf16[1024,3,1024]{2,0,1:T(8,128)(2,1)}, bf16[1024,1024]{1,0:T(8,128)(2,1)}), (bf16[1024,3,1024]{2,0,1:T(8,128)(2,1)}, bf16[1024,1024]{1,0:T(8,128)(2,1)})) %all-reduce.15.cloned.1.call-update) | async-done | bytes 8388624 | tf_op jit(solution)/shard_map/psum | solution.py:20
  274.5 0.0 copy-start.1
  274.5 0.0 copy-start.2
  274.5 3.3 convert_multiply_fusion.1
  277.9 0.7 copy-done.1
  278.6 0.6 copy-done.2
  279.2 5.2 %multiply_reduce_fusion = (f32[1024]{0:T(1024)S(1)}, f32[1024]{0:T(1024)S(1)}, f32[1024]{0:T(1024)S(1)}, f32[1024]{0:T(1024)S(1)}, f32[1024]{0:T(1024)S(1)}, /*i...) fusion(f32[1018,1024]{1,0:T(8,128)S(1)} %bitcast.96, bf16[1024,3,1024]{2,0,1:T(8,128)(2,1)S(1)} %copy-done.1, ...), kind=kLoop, calls=%fused_computation.12 | loop fusion | flops 20964352 | bytes 37691392 | tf_op jit(solution)/shard_map/reduce_sum | solution.py:75
  284.4 2.5 slice.114
  286.9 2.5 slice.113
  289.4 2.5 slice.112
  292.0 2.6 slice.111
  294.5 2.5 slice.110
  297.0 2.6 slice.115
  299.6 13.3 %fusion.2 = (bf16[1024,1,1024]{2,0,1:T(8,128)(2,1)}, f32[1024,1024]{1,0:T(8,128)}) fusion(bf16[1024,3,1024]{2,0,1:T(8,128)(2,1)S(1)} %copy-done.1, f32[1018,1024]{1,0:T(8,128)} %slice.115, f32[1024]{0:T(1024)S(1)} %bitcast.122, f32[1019,1024]{1,0:T(8,128)} %slice.114, f32[1024]{0:T(1024)S(1)} %bitcast.124, f32[1020,1024]{1,0:T(8,128)} %slice.113, ...), kind=kLoop, calls=%fused_computation.10 | loop fusion | flops 19922944 | bytes 37691392 | tf_op jit(solution)/shard_map/stack | solution.py:82
  312.8 9.9 %fusion = (bf16[1024,1,1024]{2,0,1:T(8,128)(2,1)}, f32[1024,1024]{1,0:T(8,128)}, bf16[1024,1,1024]{2,0,1:T(8,128)(2,1)}) fusion(bf16[1024,1024]{1,0:T(8,128)(2,1)} %get-tuple-element.23, f32[1018,1024]{1,0:T(8,128)S(1)} %bitcast.102, f32[1024]{0:T(1024)S(1)} %bitcast.123, f32[1019,1024]{1,0:T(8,128)S(1)} %bitcast.103, f32[1024]{0:T(1024)S(1)} %bitcast.125, ...), kind=kLoop, calls=%fused_computation.8 | loop fusion | flops 22020096 | bytes 43982848 | tf_op jit(solution)/shard_map/stack | solution.py:82
  322.7 0.0 copy-start.3
  322.7 3.9 convolution_convert_fusion.2
  326.6 0.0 reduce-scatter.3.cloned.1.call-update
  326.6 0.3 reduce-scatter.5.cloned.1.call-start
  326.9 0.0 copy-done.3
  326.9 5.5 %maximum_convert_fusion = bf16[1024,3,1024]{2,0,1:T(8,128)(2,1)} fusion(bf16[1024,1,1024]{2,0,1:T(8,128)(2,1)} %get-tuple-element.29, bf16[1024,1,1024]{2,0,1:T(8,128)(2,1)S(1)} %copy-done.3, bf16[1024,1,1024]{2,0,1:T(8,128)(2,1)} %get-tuple-element.24), kind=kLoop, calls=%fused_computation | loop fusion | flops 6291456 | bytes 12582912 | tf_op jit(solution)/shard_map/convert_element_type | solution.py:84
  332.5 0.0 copy-start.8
  332.5 8.8 %copy.15 = bf16[1024,3,1024]{0,2,1:T(8,128)(2,1)} copy(bf16[1024,3,1024]{2,0,1:T(8,128)(2,1)} %maximum_convert_fusion) | data formatting | bytes 12582912 | tf_op jit(solution)/shard_map/convert_element_type | solution.py:84
  341.3 0.0 copy-done.8
  341.3 0.0 copy-start.7
  341.3 5.5 %fusion.5 = bf16[1024,256]{1,0:T(8,128)(2,1)} fusion(bf16[1024,3,1024]{2,0,1:T(8,128)(2,1)} %maximum_convert_fusion, bf16[256,3,1024]{2,0,1:T(8,128)(2,1)S(1)} %copy-done.8), kind=kOutput, calls=%fused_computation.29 | convolution fusion | flops 1610874880 | bytes 8388608 | tf_op jit(solution)/shard_map/dot_general | solution.py:97
  346.8 0.0 reduce-scatter.5.cloned.1.call-update
  346.8 0.0 copy-done.7
  346.9 0.0 copy-start.5
  346.9 4.7 %fusion.4 = bf16[3072,256]{1,0:T(8,128)(2,1)S(1)} fusion(bf16[1024,3072]{0,1:T(8,128)(2,1)} %bitcast.109, bf16[1024,256]{1,0:T(8,128)(2,1)S(1)} %copy-done.7), kind=kOutput, calls=%fused_computation.22 | convolution fusion | flops 1612185600 | bytes 8388608 | tf_op jit(solution)/shard_map/dot_general | solution.py:88
  351.5 1.7 copy.16
  353.3 0.0 copy-start.9
  353.3 0.0 copy-start.10
  353.3 0.1 stack.47
  353.3 0.7 dynamic-slice_multiply_fusion
  354.0 0.0 copy-done.5
  354.0 4.7 %fusion.6 = bf16[1024,256]{1,0:T(8,128)(2,1)} fusion(bf16[1024,256]{1,0:T(8,128)(2,1)S(1)} %copy-done.5, f32[1024,1024]{1,0:T(8,128)} %get-tuple-element.25, bf16[1024,3,1024]{2,0,1:T(8,128)(2,1)} %get-tuple-element.22), kind=kOutput, calls=%fused_computation.31 | convolution fusion | flops 540540928 | bytes 7340032 | tf_op jit(solution)/shard_map/dot_general | solution.py:60
  358.7 0.6 reduce-scatter.3.cloned.1.call-done
  359.4 0.0 copy-done.9
  359.4 1.5 add_convert_fusion.1
  360.9 33.7 %reduce-scatter.5.cloned.1.call-done = bf16[128,256]{1,0:T(8,128)(2,1)} async-done(((bf16[1024,256]{1,0:T(8,128)(2,1)}), bf16[128,256]{1,0:T(8,128)(2,1)}) %reduce-scatter.5.cloned.1.call-update) | async-done | bytes 65552 | tf_op jit(solution)/shard_map/reduce_scatter | solution.py:14
  394.6 0.0 copy-done.10
  394.6 1.5 add_convert_fusion
  (1 shorter events, 0.0 us)
Async XLA Ops:
  7.2 51.1 %copy-start = (bf16[1024,256]{1,0:T(8,128)(2,1)S(1)}, bf16[1024,256]{1,0:T(8,128)(2,1)}, u32[]{:S(2)}) copy-start(bf16[1024,256]{1,0:T(8,128)(2,1)} %param.8) | copy-start | bytes 1572868
  7.2 267.4 %all-reduce.15.cloned.1.call-start = ((), (), s32[]{:S(2)}) async-start(), calls=%async_computation.4 | async-start | bytes 16777216 | tf_op jit(solution)/shard_map/psum | solution.py:20
  21.2 19.7 %copy-start.6 = (bf16[1024,256]{1,0:T(8,128)(2,1)}, bf16[1024,256]{1,0:T(8,128)(2,1)S(1)}, u32[]{:S(2)}) copy-start(bf16[1024,256]{1,0:T(8,128)(2,1)S(1)} %all_gather.6) | copy-start | bytes 1572868
  34.5 23.8 %copy-start.4 = (bf16[1024,256]{1,0:T(8,128)(2,1)}, bf16[1024,256]{1,0:T(8,128)(2,1)S(1)}, u32[]{:S(2)}) copy-start(bf16[1024,256]{1,0:T(8,128)(2,1)S(1)} %all_gather.7) | copy-start | bytes 1572868
  60.4 0.8 copy-start.11
  60.4 298.9 %reduce-scatter.3.cloned.1.call-start = ((), (), s32[]{:S(2)}) async-start(), calls=%async_computation.2 | async-start | bytes 589824 | tf_op jit(solution)/shard_map/reduce_scatter | solution.py:14
  274.5 4.0 %copy-start.1 = (bf16[1024,3,1024]{2,0,1:T(8,128)(2,1)S(1)}, bf16[1024,3,1024]{2,0,1:T(8,128)(2,1)}, u32[]{:S(2)}) copy-start(bf16[1024,3,1024]{2,0,1:T(8,128)(2,1)} %get-tuple-element.22) | copy-start | bytes 18874372
  274.5 4.7 %copy-start.2 = (bf16[1024,1024]{1,0:T(8,128)(2,1)S(1)}, bf16[1024,1024]{1,0:T(8,128)(2,1)}, u32[]{:S(2)}) copy-start(bf16[1024,1024]{1,0:T(8,128)(2,1)} %get-tuple-element.23) | copy-start | bytes 6291460
  322.7 4.2 %copy-start.3 = (bf16[1024,1,1024]{2,0,1:T(8,128)(2,1)S(1)}, bf16[1024,1,1024]{2,0,1:T(8,128)(2,1)}, u32[]{:S(2)}) copy-start(bf16[1024,1,1024]{2,0,1:T(8,128)(2,1)} %get-tuple-element.26) | copy-start | bytes 6291460
  326.6 67.9 %reduce-scatter.5.cloned.1.call-start = ((), (), s32[]{:S(2)}) async-start(), calls=%async_computation.3 | async-start | bytes 589824 | tf_op jit(solution)/shard_map/reduce_scatter | solution.py:14
  332.5 8.8 %copy-start.8 = (bf16[256,3,1024]{2,0,1:T(8,128)(2,1)S(1)}, bf16[256,3,1024]{2,0,1:T(8,128)(2,1)}, u32[]{:S(2)}) copy-start(bf16[256,3,1024]{2,0,1:T(8,128)(2,1)} %param.7) | copy-start | bytes 4718596
  341.3 5.6 %copy-start.7 = (bf16[1024,256]{1,0:T(8,128)(2,1)S(1)}, bf16[1024,256]{1,0:T(8,128)(2,1)}, u32[]{:S(2)}) copy-start(bf16[1024,256]{1,0:T(8,128)(2,1)} %copy-done.6) | copy-start | bytes 1572868
  346.9 7.2 %copy-start.5 = (bf16[1024,256]{1,0:T(8,128)(2,1)S(1)}, bf16[1024,256]{1,0:T(8,128)(2,1)}, u32[]{:S(2)}) copy-start(bf16[1024,256]{1,0:T(8,128)(2,1)} %copy-done.4) | copy-start | bytes 1572868
  353.3 6.1 %copy-start.9 = (bf16[128,256]{1,0:T(8,128)(2,1)S(1)}, bf16[128,256]{1,0:T(8,128)(2,1)}, u32[]{:S(2)}) copy-start(bf16[128,256]{1,0:T(8,128)(2,1)} %param.5) | copy-start | bytes 196612
  353.3 41.3 %copy-start.10 = (bf16[128,256]{1,0:T(8,128)(2,1)S(1)}, bf16[128,256]{1,0:T(8,128)(2,1)}, u32[]{:S(2)}) copy-start(bf16[128,256]{1,0:T(8,128)(2,1)} %param.6) | copy-start | bytes 196612
Sparse Core Ops, SparseCore 0:
  60.5 213.9 all-reduce.14
  326.8 32.5 reduce-scatter.2
  361.9 32.6 reduce-scatter.4

commit v2 on v1

v2 whole, which is shorter than its diff:
```python
import math

import jax
import jax.numpy as jnp
from jax import lax
from jax.experimental import pallas as pl
from jax.experimental.pallas import tpu as pltpu
from jax.sharding import PartitionSpec as P


def rows_in(operand):
    return lax.all_gather(operand, "row", axis=0, tiled=True)


def fold_rows(summand):
    return lax.psum_scatter(
        summand.astype(jnp.bfloat16), "row", scatter_dimension=0, tiled=True
    ).astype(jnp.float32)


def sum_cols(summand):
    return lax.psum(summand.astype(jnp.bfloat16), "col")


def gate_body(q_ref, k_ref, v_ref, g_ref, t_ref, gated_ref, gq_ref, gk_ref, gv_ref, ts_ref):
    tokens, width = q_ref.shape
    kernel_len = t_ref.shape[0]
    q = q_ref[...].astype(jnp.float32)
    k = k_ref[...].astype(jnp.float32)
    v = v_ref[...].astype(jnp.float32)
    g = g_ref[...].astype(jnp.float32)
    taps = t_ref[...]
    row = lax.broadcasted_iota(jnp.int32, (tokens, width), 0)
    kv = k * v
    kv_lag = [kv]
    for i in range(1, kernel_len):
        kv_lag.append(jnp.where(row >= i, pltpu.roll(kv, i, 0), 0.0))
    conv = jnp.zeros_like(kv)
    for i in range(kernel_len):
        conv = conv + taps[i : i + 1, :] * kv_lag[i]
    gated_ref[...] = (q * conv).astype(gated_ref.dtype)
    gc = g * q
    gp = jnp.zeros_like(gc)
    sums = []
    for i in range(kernel_len):
        if i == 0:
            lead = gc
        else:
            lead = jnp.where(row < tokens - i, pltpu.roll(gc, tokens - i, 0), 0.0)
        gp = gp + taps[i : i + 1, :] * lead
        sums.append(jnp.sum(gc * kv_lag[i], axis=0, keepdims=True))
    sums.append(jnp.zeros((ts_ref.shape[0] - kernel_len, width), jnp.float32))
    ts_ref[...] = jnp.concatenate(sums, 0)
    gq_ref[...] = (g * conv).astype(gq_ref.dtype)
    gk_ref[...] = (gp * v).astype(gk_ref.dtype)
    gv_ref[...] = (gp * k).astype(gv_ref.dtype)


def gate_kernel(mixed_flat, grad_gated, taps_t, width=128):
    tokens, three_ch = mixed_flat.shape
    channels = three_ch // 3
    kernel_len = taps_t.shape[0]
    tiles = channels // width
    col = lambda off: pl.BlockSpec((tokens, width), lambda j: (0, j + off))
    half = jax.ShapeDtypeStruct((tokens, channels), jnp.bfloat16)
    return pl.pallas_call(
        gate_body,
        grid=(tiles,),
        in_specs=[
            col(0),
            col(tiles),
            col(2 * tiles),
            col(0),
            pl.BlockSpec((kernel_len, width), lambda j: (0, j)),
        ],
        out_specs=[col(0), col(0), col(0), col(0), pl.BlockSpec((8, width), lambda j: (0, j))],
        out_shape=[half, half, half, half, jax.ShapeDtypeStruct((8, channels), jnp.float32)],
        cost_estimate=pl.CostEstimate(
            flops=60 * tokens * channels, transcendentals=0, bytes_accessed=18 * tokens * channels
        ),
    )(mixed_flat, mixed_flat, mixed_flat, grad_gated, taps_t)


def on_device(inputs, out_grad, in_weight, out_weight, filter_taps):
    col_width = inputs.shape[1]
    row_width = out_weight.shape[0]
    weight_flat = in_weight.reshape(col_width, 3 * row_width)
    whole_in = rows_in(inputs)
    all_tokens = whole_in.shape[0]
    grad_scale = 1.0 / math.sqrt(all_tokens)

    in_term = jnp.dot(whole_in, weight_flat, preferred_element_type=jnp.float32)
    whole_grad = rows_in(out_grad)
    dy_term = lax.dot_general(
        whole_grad, out_weight, (((1,), (1,)), ((), ())), preferred_element_type=jnp.float32
    )
    mixed_flat = sum_cols(in_term)
    grad_gated = sum_cols(dy_term)
    gated_all, grad_query, grad_key, grad_value, tap_sums = gate_kernel(
        mixed_flat, grad_gated, filter_taps.T
    )

    projected = fold_rows(
        jnp.dot(gated_all, out_weight, preferred_element_type=jnp.float32)
    )
    result = (inputs.astype(jnp.float32) + projected).astype(jnp.bfloat16)
    out_w_grad = (
        lax.dot_general(
            gated_all, whole_grad, (((0,), (0,)), ((), ())), preferred_element_type=jnp.float32
        )
        * grad_scale
    ).astype(jnp.bfloat16)
    cols = lax.axis_size("col")
    own = row_width // cols
    kernel_len = filter_taps.shape[1]
    filter_grad = (
        lax.dynamic_slice_in_dim(tap_sums[:kernel_len], lax.axis_index("col") * own, own, 1).T
        * grad_scale
    )
    grad_flat = jnp.concatenate([grad_query, grad_key, grad_value], axis=1)
    in_grad = (
        (
            lax.dot_general(
                whole_in, grad_flat, (((0,), (0,)), ((), ())), preferred_element_type=jnp.float32
            )
            * grad_scale
        )
        .astype(jnp.bfloat16)
        .reshape(col_width, 3, row_width)
    )
    back_sum = fold_rows(
        lax.dot_general(
            grad_flat, weight_flat, (((1,), (1,)), ((), ())), preferred_element_type=jnp.float32
        )
    )
    input_grad = (out_grad.astype(jnp.float32) + back_sum).astype(jnp.bfloat16)
    return (result, input_grad, in_grad, out_w_grad, filter_grad)


def solution(mesh):
    placed = (
        P("row", "col"),
        P("row", "col"),
        P("col", None, "row"),
        P("row", "col"),
        P("row", None),
    )
    return jax.shard_map(
        on_device,
        mesh=mesh,
        in_specs=placed,
        out_specs=(
            P("row", "col"),
            P("row", "col"),
            P("col", None, "row"),
            P("row", "col"),
            P(("row", "col"), None),
        ),
        check_vma=False,
    )
```

time: 404 us -> 351 us (0.87)
  local copies, waits for them, and re-layouts: 46.9 us -> 10.1 us
  other arithmetic: 40.8 us -> 4.32 us
  Pallas kernels: 0 us -> 14 us
  waiting for transfers between devices: 248 us -> 260 us
  matrix products: 25.4 us -> 20.2 us
    another operation x2 -> x0, other arithmetic: 23.1 us -> none  [on_device(): jnp.stack([grad_query, grad_product * value_part, grad_product * key_part...]
    convert_element_type x2 -> x0, local copies, waits for them, and re-layouts: 17.5 us -> none  [the longest x1 8.83 us: on_device(): grad_mixed = jnp.stack([grad_query, grad_product * value_part, grad_produ...]
    slice x7 -> x0, local copies, waits for them, and re-layouts: 15.1 us -> none  [the longest x6 15.1 us: shifted(): return jnp.concatenate([values[-by:], pad], 0)]
    pallas_call x0 -> x1, Pallas kernels: none -> 14 us  [gate_kernel(): pl.pallas_call(gate_body, grid=(tiles,), in_specs=[col(0), col(tiles), co...]
    reduce_scatter x2, waiting for transfers between devices: 34.4 us -> 46.2 us  [fold_rows(): lax.psum_scatter(summand.astype(jnp.bfloat16), 'row', scatter_dimension=0...]
    reshape x1 -> x0, local copies, waits for them, and re-layouts: 8.7 us -> none  [on_device(): mixed_qkv = sum_cols(in_term).reshape(all_tokens, 3, row_width)]
    convert_element_type x1 -> x0, other arithmetic: 5.52 us -> none  [on_device(): grad_mixed = jnp.stack([grad_query, grad_product * value_part, grad_produ...]
    reduce_sum x1 -> x0, other arithmetic: 5.22 us -> none  [on_device(): tap_terms.append(jnp.sum(grad_conv * shifted(kv_product, offset), axis=0))]
  transfers between devices with their start and end apart: 3 -> 3, of which waited for: 3 -> 3; matrix products, arithmetic and copies ran while one was open for 8% -> 5% of each run, Pallas kernels for 0% -> 0%
where the time goes in v2:
time: 351 us; the launch traced here: 350 us
  waiting for transfers between devices  260 us (74%)
  blocking collectives  27.3 us (8%)
  matrix products  20.2 us (6%)
  Pallas kernels  14 us (4%)
  between operations  13.8 us (4%)
  local copies, waits for them, and re-layouts  10.1 us (3%)
  other arithmetic  4.32 us (1%)
    psum x1, waiting for transfers between devices, sum_cols(): return lax.psum(summand.astype(jnp.bfloat16), 'col')  214 us
    reduce_scatter x2, waiting for transfers between devices, fold_rows(): lax.psum_scatter(summand.astype(jnp.bfloat16), 'row', scatter_dimension=0...  46.2 us
    all_gather x2, blocking collectives, rows_in(): return lax.all_gather(operand, 'row', axis=0, tiled=True)  27.3 us
    pallas_call x1, Pallas kernels, gate_kernel(): pl.pallas_call(gate_body, grid=(tiles,), in_specs=[col(0), col(tiles), co...  14 us
    unnamed x16, local copies, waits for them, and re-layouts  9.91 us
  transfers between devices with their start and end apart: 3, of which 3 were waited for; matrix products, arithmetic and copies ran while one was open for 5% of the time, Pallas kernels for 0%

profile of v2, /device:TPU:2, one launch (start us, length us, event | category | flops | bytes accessed | tf_op | source)
XLA Modules:
  0.0 350.2 jit_solution(13130097487505721160)
XLA Ops:
  7.2 0.0 copy-start
  7.2 0.0 all-reduce.3.cloned.1.call-start
  7.2 14.0 %all_gather.6 = bf16[1024,256]{1,0:T(8,128)(2,1)S(1)} all-gather(bf16[128,256]{1,0:T(8,128)(2,1)} %param.5), channel_id=1, replica_groups=mesh['row'=8,'col'=32] {'row'}, dimensions={0}, use_global_device_ids=true | all-gather | bytes 589824 | tf_op jit(solution)/shard_map/all_gather | solution.py:12
  21.2 13.3 %all_gather.7 = bf16[1024,256]{1,0:T(8,128)(2,1)S(1)} all-gather(bf16[128,256]{1,0:T(8,128)(2,1)} %param.6), channel_id=1, replica_groups=mesh['row'=8,'col'=32] {'row'}, dimensions={0}, use_global_device_ids=true | all-gather | bytes 589824 | tf_op jit(solution)/shard_map/all_gather | solution.py:12
  34.5 1.7 copy.11
  36.2 0.0 copy-done
  36.2 2.0 convolution_convert_fusion.1
  38.3 4.5 %convolution_convert_fusion = bf16[1024,3072]{1,0:T(8,128)(2,1)} fusion(bf16[1024,256]{1,0:T(8,128)(2,1)S(1)} %all_gather.6, bf16[256,3072]{0,1:T(8,128)(2,1)S(1)} %bitcast.20), kind=kOutput, calls=%fused_computation | convolution fusion | flops 1613758464 | bytes 8388608 | tf_op jit(solution)/shard_map/dot_general | solution.py:92
  42.8 0.0 all-reduce.3.cloned.1.call-update
  42.8 0.0 reduce-scatter.3.cloned.1.call-start
  42.8 214.2 %all-reduce.3.cloned.1.call-done = (bf16[1024,3072]{1,0:T(8,128)(2,1)}, bf16[1024,1024]{1,0:T(8,128)(2,1)}) async-done(((bf16[1024,3072]{1,0:T(8,128)(2,1)}, bf16[1024,1024]{1,0:T(8,128)(2,1)}), (bf16[1024,3072]{1,0:T(8,128)(2,1)}, bf16[1024,1024]{1,0:T(8,128)(2,1)})) %all-reduce.3.cloned.1.call-update) | async-done | bytes 8388624 | tf_op jit(solution)/shard_map/psum | solution.py:22
  257.0 14.0 %shard_map.92 = (bf16[1024,1024]{1,0:T(8,128)(2,1)}, bf16[1024,1024]{1,0:T(8,128)(2,1)}, bf16[1024,1024]{1,0:T(8,128)(2,1)}, bf16[1024,1024]{1,0:T(8,128)(2,1)}, f32[8,1024]{1,0:T(8,128)}) custom-call(bf16[1024,3072]{1,0:T(8,128)(2,1)} %get-tuple-element.25.q_ref.k_ref.v_ref, bf16[1024,3072]{1,0:T(8,128)(2,1)} %get-tuple-element.25.q_ref.k_ref.v_ref, ...), custom_call_target="tpu_custom_call" | custom-call | flops 62914560 | bytes 18874368 | tf_op jit(solution)/shard_map/pallas_call | solution.py:66
  270.9 3.1 convolution_convert_fusion.3
  274.1 0.0 reduce-scatter.3.cloned.1.call-update
  274.1 0.0 reduce-scatter.5.cloned.1.call-start
  274.1 0.0 copy-start.2
  274.1 1.9 constant_dynamic-update-slice_fusion.2
  276.1 0.3 copy-done.2
  276.4 0.0 copy-start.1
  276.4 0.2 constant_dynamic-update-slice_fusion.1
  276.5 1.4 copy-done.1
  277.9 0.2 constant_dynamic-update-slice_fusion
  278.1 0.0 copy-start.3
  278.1 2.7 copy-done.3
  280.8 2.6 convolution_convert_fusion.2
  283.4 0.0 reduce-scatter.5.cloned.1.call-update
  283.5 4.7 %fusion = bf16[3072,256]{1,0:T(8,128)(2,1)S(1)} fusion(bf16[1024,3072]{1,0:T(8,128)(2,1)} %copy-done.3, bf16[1024,256]{1,0:T(8,128)(2,1)S(1)} %all_gather.6), kind=kOutput, calls=%fused_computation.2 | convolution fusion | flops 1612185600 | bytes 8388608 | tf_op jit(solution)/shard_map/dot_general | solution.py:123
  288.2 1.7 copy.12
  289.9 1.4 multiply_bitcast_fusion
  291.3 0.0 copy-start.4
  291.3 0.0 copy-start.5
  291.3 3.2 fusion.1
  294.5 12.3 %reduce-scatter.3.cloned.1.call-done = bf16[128,256]{1,0:T(8,128)(2,1)} async-done(((bf16[1024,256]{1,0:T(8,128)(2,1)}), bf16[128,256]{1,0:T(8,128)(2,1)}) %reduce-scatter.3.cloned.1.call-update) | async-done | bytes 65552 | tf_op jit(solution)/shard_map/reduce_scatter | solution.py:16
  306.8 0.0 copy-done.4
  306.8 1.5 add_convert_fusion.1
  308.3 33.8 %reduce-scatter.5.cloned.1.call-done = bf16[128,256]{1,0:T(8,128)(2,1)} async-done(((bf16[1024,256]{1,0:T(8,128)(2,1)}), bf16[128,256]{1,0:T(8,128)(2,1)}) %reduce-scatter.5.cloned.1.call-update) | async-done | bytes 65552 | tf_op jit(solution)/shard_map/reduce_scatter | solution.py:16
  342.1 0.0 copy-done.5
  342.1 1.5 add_convert_fusion
Async XLA Ops:
  7.2 29.1 %copy-start = (bf16[1024,256]{1,0:T(8,128)(2,1)S(1)}, bf16[1024,256]{1,0:T(8,128)(2,1)}, u32[]{:S(2)}) copy-start(bf16[1024,256]{1,0:T(8,128)(2,1)} %param.8) | copy-start | bytes 1572868
  7.2 249.8 %all-reduce.3.cloned.1.call-start = ((), (), s32[]{:S(2)}) async-start(), calls=%async_computation.4 | async-start | bytes 16777216 | tf_op jit(solution)/shard_map/psum | solution.py:22
  42.8 264.0 %reduce-scatter.3.cloned.1.call-start = ((), (), s32[]{:S(2)}) async-start(), calls=%async_computation.2 | async-start | bytes 589824 | tf_op jit(solution)/shard_map/reduce_scatter | solution.py:16
  274.1 68.1 %reduce-scatter.5.cloned.1.call-start = ((), (), s32[]{:S(2)}) async-start(), calls=%async_computation.3 | async-start | bytes 589824 | tf_op jit(solution)/shard_map/reduce_scatter | solution.py:16
  274.1 2.2 copy-start.2
  276.4 1.6 copy-start.1
  278.1 2.7 copy-start.3
  291.3 15.5 %copy-start.4 = (bf16[128,256]{1,0:T(8,128)(2,1)S(1)}, bf16[128,256]{1,0:T(8,128)(2,1)}, u32[]{:S(2)}) copy-start(bf16[128,256]{1,0:T(8,128)(2,1)} %param.5) | copy-start | bytes 196612
  291.3 50.8 %copy-start.5 = (bf16[128,256]{1,0:T(8,128)(2,1)S(1)}, bf16[128,256]{1,0:T(8,128)(2,1)}, u32[]{:S(2)}) copy-start(bf16[128,256]{1,0:T(8,128)(2,1)} %param.6) | copy-start | bytes 196612
Sparse Core Ops, SparseCore 0:
  42.9 214.0 all-reduce.2
  274.2 32.5 reduce-scatter.2
  309.3 32.7 reduce-scatter.4

commit v3 on v2

--- a/solution.py
+++ b/solution.py
@@ -85,12 +85,13 @@
     col_width = inputs.shape[1]
     row_width = out_weight.shape[0]
     weight_flat = in_weight.reshape(col_width, 3 * row_width)
-    whole_in = rows_in(inputs)
+    both_in = rows_in(jnp.concatenate([inputs, out_grad], axis=1))
+    whole_in = both_in[:, :col_width]
+    whole_grad = both_in[:, col_width:]
     all_tokens = whole_in.shape[0]
     grad_scale = 1.0 / math.sqrt(all_tokens)
 
     in_term = jnp.dot(whole_in, weight_flat, preferred_element_type=jnp.float32)
-    whole_grad = rows_in(out_grad)
     dy_term = lax.dot_general(
         whole_grad, out_weight, (((1,), (1,)), ((), ())), preferred_element_type=jnp.float32
     )
@@ -100,10 +101,7 @@
         mixed_flat, grad_gated, filter_taps.T
     )
 
-    projected = fold_rows(
-        jnp.dot(gated_all, out_weight, preferred_element_type=jnp.float32)
-    )
-    result = (inputs.astype(jnp.float32) + projected).astype(jnp.bfloat16)
+    projected_term = jnp.dot(gated_all, out_weight, preferred_element_type=jnp.float32)
     out_w_grad = (
         lax.dot_general(
             gated_all, whole_grad, (((0,), (0,)), ((), ())), preferred_element_type=jnp.float32
@@ -128,11 +126,13 @@
         .astype(jnp.bfloat16)
         .reshape(col_width, 3, row_width)
     )
-    back_sum = fold_rows(
-        lax.dot_general(
-            grad_flat, weight_flat, (((1,), (1,)), ((), ())), preferred_element_type=jnp.float32
-        )
+    back_term = lax.dot_general(
+        grad_flat, weight_flat, (((1,), (1,)), ((), ())), preferred_element_type=jnp.float32
     )
+    both_sums = fold_rows(jnp.concatenate([projected_term, back_term], axis=1))
+    projected = both_sums[:, :col_width]
+    back_sum = both_sums[:, col_width:]
+    result = (inputs.astype(jnp.float32) + projected).astype(jnp.bfloat16)
     input_grad = (out_grad.astype(jnp.float32) + back_sum).astype(jnp.bfloat16)
     return (result, input_grad, in_grad, out_w_grad, filter_grad)
 

time: 351 us -> 326 us (0.929)
  blocking collectives: 27.3 us -> 0 us
  local copies, waits for them, and re-layouts: 10.1 us -> 14.1 us
    reduce_scatter x2 -> x0, waiting for transfers between devices: 46.2 us -> none  [fold_rows(): lax.psum_scatter(summand.astype(jnp.bfloat16), 'row', scatter_dimension=0...]
    all_gather x0 -> x1, waiting for transfers between devices: none -> 28.6 us  [rows_in(): return lax.all_gather(operand, 'row', axis=0, tiled=True)]
    all_gather x2 -> x0, blocking collectives: 27.3 us -> none  [rows_in(): return lax.all_gather(operand, 'row', axis=0, tiled=True)]
    unnamed x3 -> x4, waiting for transfers between devices: 0.05 us -> 20.1 us
    unnamed x16 -> x26, local copies, waits for them, and re-layouts: 9.91 us -> 12.3 us
where the time goes in v3:
time: 326 us; the launch traced here: 325 us
  waiting for transfers between devices  261 us (80%)
  matrix products  19.8 us (6%)
  local copies, waits for them, and re-layouts  14.1 us (4%)
  Pallas kernels  13.9 us (4%)
  between operations  13.9 us (4%)
    psum x1, waiting for transfers between devices, sum_cols(): return lax.psum(summand.astype(jnp.bfloat16), 'col')  212 us
    all_gather x1, waiting for transfers between devices, rows_in(): return lax.all_gather(operand, 'row', axis=0, tiled=True)  28.6 us
    unnamed x4, waiting for transfers between devices  20.1 us
    pallas_call x1, Pallas kernels, gate_kernel(): pl.pallas_call(gate_body, grid=(tiles,), in_specs=[col(0), col(tiles), co...  13.9 us
    unnamed x26, local copies, waits for them, and re-layouts  12.3 us
  transfers between devices with their start and end apart: 3, of which 3 were waited for; matrix products, arithmetic and copies ran while one was open for 5% of the time, Pallas kernels for 0%

profile of v3, /device:TPU:2, one launch (start us, length us, event | category | flops | bytes accessed | tf_op | source)
XLA Modules:
  0.0 325.5 jit_solution(1076901310823528172)
XLA Ops:
  7.2 0.0 copy-start
  7.2 0.0 all-gather.2.cloned.1.call-start
  7.2 1.6 pad_maximum_fusion.1
  8.8 0.0 all-gather.2.cloned.1.call-update
  8.8 0.0 all-reduce.3.cloned.1.call-start
  8.9 1.7 copy.23
  10.6 28.6 %all-gather.2.cloned.1.call-done = bf16[1024,512]{1,0:T(8,128)(2,1)} async-done(((bf16[128,512]{1,0:T(8,128)(2,1)}), bf16[1024,512]{1,0:T(8,128)(2,1)}) %all-gather.2.cloned.1.call-update) | async-done | bytes 1048592 | tf_op jit(solution)/shard_map/all_gather | solution.py:12
  39.2 0.0 copy-done
  39.2 0.0 copy-start.2
  39.2 3.2 convolution_convert_fusion.1
  42.4 0.0 copy-done.2
  42.4 4.5 %convolution_convert_fusion = bf16[1024,3072]{1,0:T(8,128)(2,1)} fusion(bf16[256,3072]{0,1:T(8,128)(2,1)S(1)} %bitcast.16, bf16[1024,512]{1,0:T(8,128)(2,1)S(1)} %copy-done.2), kind=kOutput, calls=%fused_computation | convolution fusion | flops 1613758464 | bytes 8388608 | tf_op jit(solution)/shard_map/dot_general | solution.py:94
  46.9 0.0 all-reduce.3.cloned.1.call-update
  46.9 0.0 reduce-scatter.4.cloned.1.call-start
  47.0 211.8 %all-reduce.3.cloned.1.call-done = (bf16[1024,3072]{1,0:T(8,128)(2,1)}, bf16[1024,1024]{1,0:T(8,128)(2,1)}) async-done(((bf16[1024,3072]{1,0:T(8,128)(2,1)}, bf16[1024,1024]{1,0:T(8,128)(2,1)}), (bf16[1024,3072]{1,0:T(8,128)(2,1)}, bf16[1024,1024]{1,0:T(8,128)(2,1)})) %all-reduce.3.cloned.1.call-update) | async-done | bytes 8388624 | tf_op jit(solution)/shard_map/psum | solution.py:22
  258.8 13.9 %shard_map.92 = (bf16[1024,1024]{1,0:T(8,128)(2,1)}, bf16[1024,1024]{1,0:T(8,128)(2,1)}, bf16[1024,1024]{1,0:T(8,128)(2,1)}, bf16[1024,1024]{1,0:T(8,128)(2,1)}, f32[8,1024]{1,0:T(8,128)}) custom-call(bf16[1024,3072]{1,0:T(8,128)(2,1)} %get-tuple-element.30.q_ref.k_ref.v_ref, bf16[1024,3072]{1,0:T(8,128)(2,1)} %get-tuple-element.30.q_ref.k_ref.v_ref, ...), custom_call_target="tpu_custom_call" | custom-call | flops 62914560 | bytes 18874368 | tf_op jit(solution)/shard_map/pallas_call | solution.py:66
  272.7 0.0 copy-start.5
  272.8 2.5 convolution_convert_fusion.3
  275.3 0.0 copy-done.5
  275.3 0.0 copy-start.4
  275.3 0.2 constant_dynamic-update-slice_fusion.2
  275.5 1.4 copy-done.4
  276.9 0.0 copy-start.3
  276.9 0.2 constant_dynamic-update-slice_fusion.1
  277.0 1.4 copy-done.3
  278.4 0.2 constant_dynamic-update-slice_fusion
  278.6 0.0 copy-start.1
  278.6 1.9 convolution_convert_fusion.2
  280.5 0.8 copy-done.1
  281.3 0.1 pad_maximum_fusion
  281.3 0.0 copy-start.6
  281.4 0.0 copy-start.7
  281.4 1.4 copy.29
  282.7 0.0 reduce-scatter.4.cloned.1.call-update
  282.8 0.0 copy-done.6
  282.8 0.1 copy.22
  282.9 0.0 copy-done.7
  282.9 0.1 copy.24
  283.0 4.6 %fusion = bf16[256,3072]{1,0:T(8,128)(2,1)S(1)} fusion(bf16[1024,3072]{1,0:T(8,128)(2,1)} %copy-done.1, bf16[1024,512]{1,0:T(8,128)(2,1)S(1)} %copy-done.2), kind=kOutput, calls=%fused_computation.2 | convolution fusion | flops 1612185600 | bytes 8388608 | tf_op jit(solution)/shard_map/dot_general | solution.py:121
  287.6 1.6 copy.25
  289.3 2.6 copy.28
  291.8 1.4 multiply_bitcast_fusion
  293.2 3.1 fusion.1
  296.3 20.0 %reduce-scatter.4.cloned.1.call-done = bf16[128,512]{1,0:T(8,128)(2,1)} async-done(((bf16[1024,512]{1,0:T(8,128)(2,1)}), bf16[128,512]{1,0:T(8,128)(2,1)}) %reduce-scatter.4.cloned.1.call-update) | async-done | bytes 131088
  316.4 1.0 copy.30
  317.5 0.7 copy.27
  318.2 0.7 copy.26
  (2 shorter events, 0.1 us)
Async XLA Ops:
  7.2 32.1 %copy-start = (bf16[1024,256]{1,0:T(8,128)(2,1)S(1)}, bf16[1024,256]{1,0:T(8,128)(2,1)}, u32[]{:S(2)}) copy-start(bf16[1024,256]{1,0:T(8,128)(2,1)} %param.8) | copy-start | bytes 1572868
  7.2 32.0 %all-gather.2.cloned.1.call-start = ((), (), s32[]{:S(2)}) async-start(), calls=%async_computation.1 | async-start | bytes 1179648 | tf_op jit(solution)/shard_map/all_gather | solution.py:12
  8.8 250.0 %all-reduce.3.cloned.1.call-start = ((), (), s32[]{:S(2)}) async-start(), calls=%async_computation.3 | async-start | bytes 16777216 | tf_op jit(solution)/shard_map/psum | solution.py:22
  39.2 3.2 copy-start.2
  46.9 269.5 %reduce-scatter.4.cloned.1.call-start = ((), (), s32[]{:S(2)}) async-start(), calls=%async_computation.2 | async-start | bytes 1179648
  272.7 2.5 copy-start.5
  275.3 1.6 copy-start.4
  276.9 1.6 copy-start.3
  278.6 2.7 copy-start.1
  281.3 1.4 copy-start.6
  281.4 1.5 copy-start.7
Sparse Core Ops, SparseCore 0:
  10.4 28.7 all-gather.1
  47.0 211.7 all-reduce.2
  282.9 33.4 reduce-scatter.3

commit v4 on v3

--- a/solution.py
+++ b/solution.py
@@ -9,7 +9,15 @@
 
 
 def rows_in(operand):
-    return lax.all_gather(operand, "row", axis=0, tiled=True)
+    devices = lax.axis_size("row")
+    me = lax.axis_index("row")
+    arrived = [operand]
+    for dist in range(1, devices):
+        pairs = [(i, (i + dist) % devices) for i in range(devices)]
+        arrived.append(lax.ppermute(operand, "row", pairs))
+    stacked = jnp.stack(arrived)
+    order = (me - jnp.arange(devices)) % devices
+    return stacked[order].reshape((devices * operand.shape[0],) + operand.shape[1:])
 
 
 def fold_rows(summand):

time: 326 us -> 326 us (level)
  waiting for transfers between devices: 261 us -> 248 us
  local copies, waits for them, and re-layouts: 14.1 us -> 23 us
  starting transfers between devices: 0.12 us -> 6.65 us
    all_gather x1 -> x0, waiting for transfers between devices: 28.6 us -> none  [rows_in(): return lax.all_gather(operand, 'row', axis=0, tiled=True)]
    ppermute x0 -> x7, waiting for transfers between devices: none -> 15.5 us  [rows_in(): arrived.append(lax.ppermute(operand, 'row', pairs))]
    ppermute x0 -> x7, starting transfers between devices: none -> 6.39 us  [rows_in(): arrived.append(lax.ppermute(operand, 'row', pairs))]
    unnamed x26 -> x32, local copies, waits for them, and re-layouts: 12.3 us -> 17.9 us
    unnamed x4 -> x3, waiting for transfers between devices: 20.1 us -> 20.1 us
  transfers between devices with their start and end apart: 3 -> 9, of which waited for: 3 -> 5; matrix products, arithmetic and copies ran while one was open for 5% -> 6% of each run, Pallas kernels for 0% -> 0%
where the time goes in v4:
time: 326 us
  waiting for transfers between devices  248 us (76%)
  local copies, waits for them, and re-layouts  23 us (7%)
  matrix products  18.6 us (6%)
  between operations  14.2 us (4%)
  Pallas kernels  14 us (4%)
  starting transfers between devices  6.65 us (2%)
    psum x1, waiting for transfers between devices, sum_cols(): return lax.psum(summand.astype(jnp.bfloat16), 'col')  212 us
    unnamed x3, waiting for transfers between devices  20.1 us
    unnamed x32, local copies, waits for them, and re-layouts  17.9 us
    ppermute x7, waiting for transfers between devices, rows_in(): arrived.append(lax.ppermute(operand, 'row', pairs))  15.5 us
    pallas_call x1, Pallas kernels, gate_kernel(): pl.pallas_call(gate_body, grid=(tiles,), in_specs=[col(0), col(tiles), co...  14 us
  transfers between devices with their start and end apart: 9, of which 5 were waited for; matrix products, arithmetic and copies ran while one was open for 6% of the time, Pallas kernels for 0%

profile of v4, /device:TPU:2, one launch (start us, length us, event | category | flops | bytes accessed | tf_op | source)
XLA Modules:
  0.0 325.5 jit_solution(15778813852551622405)
XLA Ops:
  7.2 0.0 copy-start
  7.2 0.0 all-reduce.3.cloned.1.call-start
  7.2 0.9 constant_dynamic-update-slice_fusion.1
  8.1 0.8 constant_dynamic-update-slice_fusion
  9.0 2.5 collective-permute-start.6
  11.4 0.7 collective-permute-start.5
  12.2 0.3 collective-permute-start.4
  12.4 2.9 collective-permute-start.3
  15.3 0.0 collective-permute-start
  15.3 0.7 bitcast_dynamic-update-slice_fusion.7
  16.0 1.7 copy.23
  17.8 4.7 %collective-permute-done = bf16[128,512]{1,0:T(8,128)(2,1)S(1)} collective-permute-done((bf16[128,512]{1,0:T(8,128)(2,1)S(1)}, bf16[128,512]{1,0:T(8,128)(2,1)S(1)}, u32[]{:S(2)}, u32[]{:S(2)}) %collective-permute-start) | collective-permute-done | bytes 131104 | tf_op jit(solution)/shard_map/ppermute | solution.py:17
  22.5 0.0 collective-permute-start.1
  22.5 0.7 bitcast_dynamic-update-slice_fusion.6
  23.2 5.5 %collective-permute-done.1 = bf16[128,512]{1,0:T(8,128)(2,1)S(1)} collective-permute-done((bf16[128,512]{1,0:T(8,128)(2,1)S(1)}, bf16[128,512]{1,0:T(8,128)(2,1)S(1)}, u32[]{:S(2)}, u32[]{:S(2)}) %collective-permute-start.1) | collective-permute-done | bytes 131104 | tf_op jit(solution)/shard_map/ppermute | solution.py:17
  28.7 0.0 collective-permute-start.2
  28.7 0.7 bitcast_dynamic-update-slice_fusion.5
  29.3 5.2 %collective-permute-done.2 = bf16[128,512]{1,0:T(8,128)(2,1)S(1)} collective-permute-done((bf16[128,512]{1,0:T(8,128)(2,1)S(1)}, bf16[128,512]{1,0:T(8,128)(2,1)S(1)}, u32[]{:S(2)}, u32[]{:S(2)}) %collective-permute-start.2) | collective-permute-done | bytes 131104 | tf_op jit(solution)/shard_map/ppermute | solution.py:17
  34.6 0.7 bitcast_dynamic-update-slice_fusion.4
  35.2 0.0 collective-permute-done.3
  35.2 0.7 bitcast_dynamic-update-slice_fusion.3
  35.9 0.0 collective-permute-done.4
  35.9 0.7 bitcast_dynamic-update-slice_fusion.2
  36.6 0.0 collective-permute-done.5
  36.6 0.7 bitcast_dynamic-update-slice_fusion.1
  37.2 0.0 collective-permute-done.6
  37.3 0.7 bitcast_dynamic-update-slice_fusion
  37.9 1.8 gather_fusion
  39.8 0.0 copy-done
  39.8 2.0 convolution_convert_fusion.1
  41.8 4.5 %convolution_convert_fusion = bf16[1024,3072]{1,0:T(8,128)(2,1)} fusion(bf16[256,3072]{0,1:T(8,128)(2,1)S(1)} %bitcast.39, bf16[1024,512]{1,0:T(8,128)(2,1)S(1)} %bitcast.35), kind=kOutput, calls=%fused_computation.1 | convolution fusion | flops 1613758464 | bytes 8388608 | tf_op jit(solution)/shard_map/dot_general | solution.py:102
  46.3 0.0 all-reduce.3.cloned.1.call-update
  46.3 0.2 reduce-scatter.4.cloned.1.call-start
  46.5 212.0 %all-reduce.3.cloned.1.call-done = (bf16[1024,3072]{1,0:T(8,128)(2,1)}, bf16[1024,1024]{1,0:T(8,128)(2,1)}) async-done(((bf16[1024,3072]{1,0:T(8,128)(2,1)}, bf16[1024,1024]{1,0:T(8,128)(2,1)}), (bf16[1024,3072]{1,0:T(8,128)(2,1)}, bf16[1024,1024]{1,0:T(8,128)(2,1)})) %all-reduce.3.cloned.1.call-update) | async-done | bytes 8388624 | tf_op jit(solution)/shard_map/psum | solution.py:30
  258.5 14.0 %shard_map.92 = (bf16[1024,1024]{1,0:T(8,128)(2,1)}, bf16[1024,1024]{1,0:T(8,128)(2,1)}, bf16[1024,1024]{1,0:T(8,128)(2,1)}, bf16[1024,1024]{1,0:T(8,128)(2,1)}, f32[8,1024]{1,0:T(8,128)}) custom-call(bf16[1024,3072]{1,0:T(8,128)(2,1)} %get-tuple-element.30.q_ref.k_ref.v_ref, bf16[1024,3072]{1,0:T(8,128)(2,1)} %get-tuple-element.30.q_ref.k_ref.v_ref, ...), custom_call_target="tpu_custom_call" | custom-call | flops 62914560 | bytes 18874368 | tf_op jit(solution)/shard_map/pallas_call | solution.py:74
  272.5 2.5 convolution_convert_fusion.3
  275.0 0.0 copy-done.4
  275.0 0.0 copy-start.3
  275.0 0.2 constant_dynamic-update-slice_fusion.4
  275.2 1.4 copy-done.3
  276.6 0.2 constant_dynamic-update-slice_fusion.3
  276.8 1.4 copy-done.2
  278.2 0.2 constant_dynamic-update-slice_fusion.2
  278.3 0.0 copy-start.1
  278.3 1.9 convolution_convert_fusion.2
  280.2 0.8 copy-done.1
  281.0 0.1 pad_maximum_fusion
  281.1 0.0 copy-start.5
  281.1 0.0 copy-start.6
  281.1 1.4 copy.29
  282.4 0.0 reduce-scatter.4.cloned.1.call-update
  282.5 0.0 copy-done.5
  282.5 0.1 copy.22
  282.6 0.0 copy-done.6
  282.6 0.1 copy.24
  282.7 4.6 %fusion = bf16[256,3072]{1,0:T(8,128)(2,1)S(1)} fusion(bf16[1024,3072]{1,0:T(8,128)(2,1)} %copy-done.1, bf16[1024,512]{1,0:T(8,128)(2,1)S(1)} %bitcast.36), kind=kOutput, calls=%fused_computation.3 | convolution fusion | flops 1612185600 | bytes 8388608 | tf_op jit(solution)/shard_map/dot_general | solution.py:129
  287.4 1.6 copy.25
  289.0 2.6 copy.28
  291.5 1.4 multiply_bitcast_fusion
  292.9 3.1 fusion.1
  296.0 20.1 %reduce-scatter.4.cloned.1.call-done = bf16[128,512]{1,0:T(8,128)(2,1)} async-done(((bf16[1024,512]{1,0:T(8,128)(2,1)}), bf16[128,512]{1,0:T(8,128)(2,1)}) %reduce-scatter.4.cloned.1.call-update) | async-done | bytes 131088
  316.1 1.0 copy.30
  317.2 0.7 copy.27
  317.9 0.7 copy.26
  (6 shorter events, 0.1 us)
Async XLA Ops:
  7.2 32.6 %copy-start = (bf16[1024,256]{1,0:T(8,128)(2,1)S(1)}, bf16[1024,256]{1,0:T(8,128)(2,1)}, u32[]{:S(2)}) copy-start(bf16[1024,256]{1,0:T(8,128)(2,1)} %param.8) | copy-start | bytes 1572868
  7.2 251.3 %all-reduce.3.cloned.1.call-start = ((), (), s32[]{:S(2)}) async-start(), calls=%async_computation.2 | async-start | bytes 16777216 | tf_op jit(solution)/shard_map/psum | solution.py:30
  9.0 28.3 %collective-permute-start.6 = (bf16[128,512]{1,0:T(8,128)(2,1)S(1)}, bf16[128,512]{1,0:T(8,128)(2,1)S(1)}, u32[]{:S(2)}, u32[]{:S(2)}) collective-permute-start(bf16[128,512]{1,0:T(8,128)(2,1)S(1)} %constant_dynamic-update-slice_fusion), channel_id=1, source_target_pairs={{0,224},{32,0},{64,32},{96,64},{128,96},{160,128},{192,160},{224,1... | collective-permute-start | bytes 393224 | tf_op jit(solution)/shard_map/ppermute | solution.py:17
  11.4 25.2 %collective-permute-start.5 = (bf16[128,512]{1,0:T(8,128)(2,1)S(1)}, bf16[128,512]{1,0:T(8,128)(2,1)S(1)}, u32[]{:S(2)}, u32[]{:S(2)}) collective-permute-start(bf16[128,512]{1,0:T(8,128)(2,1)S(1)} %constant_dynamic-update-slice_fusion), channel_id=1, source_target_pairs={{0,192},{32,224},{64,0},{96,32},{128,64},{160,96},{192,128},{224,1... | collective-permute-start | bytes 393224 | tf_op jit(solution)/shard_map/ppermute | solution.py:17
  12.2 23.8 %collective-permute-start.4 = (bf16[128,512]{1,0:T(8,128)(2,1)S(1)}, bf16[128,512]{1,0:T(8,128)(2,1)S(1)}, u32[]{:S(2)}, u32[]{:S(2)}) collective-permute-start(bf16[128,512]{1,0:T(8,128)(2,1)S(1)} %constant_dynamic-update-slice_fusion), channel_id=1, source_target_pairs={{0,160},{32,192},{64,224},{96,0},{128,32},{160,64},{192,96},{224,1... | collective-permute-start | bytes 393224 | tf_op jit(solution)/shard_map/ppermute | solution.py:17
  12.4 22.8 %collective-permute-start.3 = (bf16[128,512]{1,0:T(8,128)(2,1)S(1)}, bf16[128,512]{1,0:T(8,128)(2,1)S(1)}, u32[]{:S(2)}, u32[]{:S(2)}) collective-permute-start(bf16[128,512]{1,0:T(8,128)(2,1)S(1)} %constant_dynamic-update-slice_fusion), channel_id=1, source_target_pairs={{0,128},{32,160},{64,192},{96,224},{128,0},{160,32},{192,64},{224,... | collective-permute-start | bytes 393224 | tf_op jit(solution)/shard_map/ppermute | solution.py:17
  15.3 7.2 %collective-permute-start = (bf16[128,512]{1,0:T(8,128)(2,1)S(1)}, bf16[128,512]{1,0:T(8,128)(2,1)S(1)}, u32[]{:S(2)}, u32[]{:S(2)}) collective-permute-start(bf16[128,512]{1,0:T(8,128)(2,1)S(1)} %constant_dynamic-update-slice_fusion), channel_id=1, source_target_pairs={{0,32},{32,64},{64,96},{96,128},{128,160},{160,192},{192,224},{224... | collective-permute-start | bytes 393224 | tf_op jit(solution)/shard_map/ppermute | solution.py:17
  22.5 6.2 %collective-permute-start.1 = (bf16[128,512]{1,0:T(8,128)(2,1)S(1)}, bf16[128,512]{1,0:T(8,128)(2,1)S(1)}, u32[]{:S(2)}, u32[]{:S(2)}) collective-permute-start(bf16[128,512]{1,0:T(8,128)(2,1)S(1)} %constant_dynamic-update-slice_fusion), channel_id=1, source_target_pairs={{0,64},{32,96},{64,128},{96,160},{128,192},{160,224},{192,0},{224,... | collective-permute-start | bytes 393224 | tf_op jit(solution)/shard_map/ppermute | solution.py:17
  28.7 5.9 %collective-permute-start.2 = (bf16[128,512]{1,0:T(8,128)(2,1)S(1)}, bf16[128,512]{1,0:T(8,128)(2,1)S(1)}, u32[]{:S(2)}, u32[]{:S(2)}) collective-permute-start(bf16[128,512]{1,0:T(8,128)(2,1)S(1)} %constant_dynamic-update-slice_fusion), channel_id=1, source_target_pairs={{0,96},{32,128},{64,160},{96,192},{128,224},{160,0},{192,32},{224,... | collective-permute-start | bytes 393224 | tf_op jit(solution)/shard_map/ppermute | solution.py:17
  46.3 269.8 %reduce-scatter.4.cloned.1.call-start = ((), (), s32[]{:S(2)}) async-start(), calls=%async_computation.1 | async-start | bytes 1179648
  272.5 2.5 copy-start.4
  275.0 1.6 copy-start.3
  276.6 1.6 copy-start.2
  278.3 2.7 copy-start.1
  281.1 1.4 copy-start.5
  281.1 1.5 copy-start.6
Sparse Core Ops, SparseCore 0:
  46.4 212.0 all-reduce.2
  282.6 33.4 reduce-scatter.3

commit v5 on v3

--- a/solution.py
+++ b/solution.py
@@ -30,24 +30,28 @@
     v = v_ref[...].astype(jnp.float32)
     g = g_ref[...].astype(jnp.float32)
     taps = t_ref[...]
-    row = lax.broadcasted_iota(jnp.int32, (tokens, width), 0)
+    edge = lax.broadcasted_iota(jnp.int32, (8, width), 0)
+
+    def lagged(x, i):
+        rolled = pltpu.roll(x, i, 0)
+        return jnp.concatenate([jnp.where(edge >= i, rolled[:8], 0.0), rolled[8:]], 0)
+
+    def leading(x, i):
+        rolled = pltpu.roll(x, tokens - i, 0)
+        return jnp.concatenate([rolled[:-8], jnp.where(edge < 8 - i, rolled[-8:], 0.0)], 0)
+
     kv = k * v
-    kv_lag = [kv]
+    kv_lag = [kv] + [lagged(kv, i) for i in range(1, kernel_len)]
+    conv = taps[0:1, :] * kv_lag[0]
     for i in range(1, kernel_len):
-        kv_lag.append(jnp.where(row >= i, pltpu.roll(kv, i, 0), 0.0))
-    conv = jnp.zeros_like(kv)
-    for i in range(kernel_len):
         conv = conv + taps[i : i + 1, :] * kv_lag[i]
     gated_ref[...] = (q * conv).astype(gated_ref.dtype)
     gc = g * q
-    gp = jnp.zeros_like(gc)
+    gp = taps[0:1, :] * gc
     sums = []
     for i in range(kernel_len):
-        if i == 0:
-            lead = gc
-        else:
-            lead = jnp.where(row < tokens - i, pltpu.roll(gc, tokens - i, 0), 0.0)
-        gp = gp + taps[i : i + 1, :] * lead
+        if i > 0:
+            gp = gp + taps[i : i + 1, :] * leading(gc, i)
         sums.append(jnp.sum(gc * kv_lag[i], axis=0, keepdims=True))
     sums.append(jnp.zeros((ts_ref.shape[0] - kernel_len, width), jnp.float32))
     ts_ref[...] = jnp.concatenate(sums, 0)
@@ -56,7 +60,7 @@
     gv_ref[...] = (gp * k).astype(gv_ref.dtype)
 
 
-def gate_kernel(mixed_flat, grad_gated, taps_t, width=128):
+def gate_kernel(mixed_flat, grad_gated, taps_t, width=256):
     tokens, three_ch = mixed_flat.shape
     channels = three_ch // 3
     kernel_len = taps_t.shape[0]

time: 326 us -> 327 us (level)
  no operation moved by 1% of the time
where the time goes in v5:
time: 327 us
  waiting for transfers between devices  260 us (80%)
  matrix products  19.8 us (6%)
  Pallas kernels  15 us (5%)
  local copies, waits for them, and re-layouts  14.1 us (4%)
  between operations  13.9 us (4%)
    psum x1, waiting for transfers between devices, sum_cols(): return lax.psum(summand.astype(jnp.bfloat16), 'col')  212 us
    all_gather x1, waiting for transfers between devices, rows_in(): return lax.all_gather(operand, 'row', axis=0, tiled=True)  28.6 us
    unnamed x4, waiting for transfers between devices  20.2 us
    pallas_call x1, Pallas kernels, gate_kernel(): pl.pallas_call(gate_body, grid=(tiles,), in_specs=[col(0), col(tiles), co...  15 us
    unnamed x26, local copies, waits for them, and re-layouts  12.3 us
  transfers between devices with their start and end apart: 3, of which 3 were waited for; matrix products, arithmetic and copies ran while one was open for 5% of the time, Pallas kernels for 0%

profile of v5, /device:TPU:2, one launch (start us, length us, event | category | flops | bytes accessed | tf_op | source)
XLA Modules:
  0.0 326.7 jit_solution(3925492795437547901)
XLA Ops:
  7.2 0.0 copy-start
  7.2 0.0 all-gather.2.cloned.1.call-start
  7.2 1.6 pad_maximum_fusion.1
  8.8 0.0 all-gather.2.cloned.1.call-update
  8.8 0.0 all-reduce.3.cloned.1.call-start
  8.9 1.7 copy.23
  10.6 28.6 %all-gather.2.cloned.1.call-done = bf16[1024,512]{1,0:T(8,128)(2,1)} async-done(((bf16[128,512]{1,0:T(8,128)(2,1)}), bf16[1024,512]{1,0:T(8,128)(2,1)}) %all-gather.2.cloned.1.call-update) | async-done | bytes 1048592 | tf_op jit(solution)/shard_map/all_gather | solution.py:12
  39.2 0.0 copy-done
  39.2 0.0 copy-start.2
  39.2 3.2 convolution_convert_fusion.1
  42.4 0.0 copy-done.2
  42.4 4.5 %convolution_convert_fusion = bf16[1024,3072]{1,0:T(8,128)(2,1)} fusion(bf16[256,3072]{0,1:T(8,128)(2,1)S(1)} %bitcast.16, bf16[1024,512]{1,0:T(8,128)(2,1)S(1)} %copy-done.2), kind=kOutput, calls=%fused_computation | convolution fusion | flops 1613758464 | bytes 8388608 | tf_op jit(solution)/shard_map/dot_general | solution.py:98
  46.9 0.0 all-reduce.3.cloned.1.call-update
  46.9 0.2 reduce-scatter.4.cloned.1.call-start
  47.1 211.7 %all-reduce.3.cloned.1.call-done = (bf16[1024,3072]{1,0:T(8,128)(2,1)}, bf16[1024,1024]{1,0:T(8,128)(2,1)}) async-done(((bf16[1024,3072]{1,0:T(8,128)(2,1)}, bf16[1024,1024]{1,0:T(8,128)(2,1)}), (bf16[1024,3072]{1,0:T(8,128)(2,1)}, bf16[1024,1024]{1,0:T(8,128)(2,1)})) %all-reduce.3.cloned.1.call-update) | async-done | bytes 8388624 | tf_op jit(solution)/shard_map/psum | solution.py:22
  258.8 15.0 %shard_map.92 = (bf16[1024,1024]{1,0:T(8,128)(2,1)}, bf16[1024,1024]{1,0:T(8,128)(2,1)}, bf16[1024,1024]{1,0:T(8,128)(2,1)}, bf16[1024,1024]{1,0:T(8,128)(2,1)}, f32[8,1024]{1,0:T(8,128)}) custom-call(bf16[1024,3072]{1,0:T(8,128)(2,1)} %get-tuple-element.30.q_ref.k_ref.v_ref, bf16[1024,3072]{1,0:T(8,128)(2,1)} %get-tuple-element.30.q_ref.k_ref.v_ref, ...), custom_call_target="tpu_custom_call" | custom-call | flops 62914560 | bytes 18874368 | tf_op jit(solution)/shard_map/pallas_call | solution.py:70
  273.8 0.0 copy-start.5
  273.8 2.5 convolution_convert_fusion.3
  276.3 0.0 copy-done.5
  276.4 0.0 copy-start.4
  276.4 0.2 constant_dynamic-update-slice_fusion.2
  276.5 1.4 copy-done.4
  277.9 0.0 copy-start.3
  278.0 0.2 constant_dynamic-update-slice_fusion.1
  278.1 1.4 copy-done.3
  279.5 0.2 constant_dynamic-update-slice_fusion
  279.7 0.0 copy-start.1
  279.7 1.9 convolution_convert_fusion.2
  281.6 0.8 copy-done.1
  282.4 0.1 pad_maximum_fusion
  282.4 0.0 copy-start.6
  282.5 0.0 copy-start.7
  282.5 1.4 copy.29
  283.8 0.0 reduce-scatter.4.cloned.1.call-update
  283.9 0.0 copy-done.6
  283.9 0.1 copy.22
  284.0 0.0 copy-done.7
  284.0 0.1 copy.24
  284.1 4.6 %fusion = bf16[256,3072]{1,0:T(8,128)(2,1)S(1)} fusion(bf16[1024,3072]{1,0:T(8,128)(2,1)} %copy-done.1, bf16[1024,512]{1,0:T(8,128)(2,1)S(1)} %copy-done.2), kind=kOutput, calls=%fused_computation.2 | convolution fusion | flops 1612185600 | bytes 8388608 | tf_op jit(solution)/shard_map/dot_general | solution.py:125
  288.7 1.6 copy.25
  290.4 2.6 copy.28
  292.9 1.4 multiply_bitcast_fusion
  294.3 3.1 fusion.1
  297.4 20.1 %reduce-scatter.4.cloned.1.call-done = bf16[128,512]{1,0:T(8,128)(2,1)} async-done(((bf16[1024,512]{1,0:T(8,128)(2,1)}), bf16[128,512]{1,0:T(8,128)(2,1)}) %reduce-scatter.4.cloned.1.call-update) | async-done | bytes 131088
  317.6 1.0 copy.30
  318.7 0.7 copy.27
  319.4 0.7 copy.26
  (2 shorter events, 0.1 us)
Async XLA Ops:
  7.2 32.1 %copy-start = (bf16[1024,256]{1,0:T(8,128)(2,1)S(1)}, bf16[1024,256]{1,0:T(8,128)(2,1)}, u32[]{:S(2)}) copy-start(bf16[1024,256]{1,0:T(8,128)(2,1)} %param.8) | copy-start | bytes 1572868
  7.2 32.0 %all-gather.2.cloned.1.call-start = ((), (), s32[]{:S(2)}) async-start(), calls=%async_computation.1 | async-start | bytes 1179648 | tf_op jit(solution)/shard_map/all_gather | solution.py:12
  8.8 250.0 %all-reduce.3.cloned.1.call-start = ((), (), s32[]{:S(2)}) async-start(), calls=%async_computation.3 | async-start | bytes 16777216 | tf_op jit(solution)/shard_map/psum | solution.py:22
  39.2 3.2 copy-start.2
  46.9 270.7 %reduce-scatter.4.cloned.1.call-start = ((), (), s32[]{:S(2)}) async-start(), calls=%async_computation.2 | async-start | bytes 1179648
  273.8 2.5 copy-start.5
  276.4 1.6 copy-start.4
  277.9 1.6 copy-start.3
  279.7 2.7 copy-start.1
  282.4 1.4 copy-start.6
  282.5 1.5 copy-start.7
Sparse Core Ops, SparseCore 0:
  10.4 28.7 all-gather.1
  47.0 211.7 all-reduce.2
  284.0 33.5 reduce-scatter.3

commit v6 on v3

--- a/solution.py
+++ b/solution.py
@@ -9,12 +9,12 @@
 
 
 def rows_in(operand):
-    return lax.all_gather(operand, "row", axis=0, tiled=True)
+    return lax.all_gather(operand, "row", axis=1, tiled=True)
 
 
 def fold_rows(summand):
     return lax.psum_scatter(
-        summand.astype(jnp.bfloat16), "row", scatter_dimension=0, tiled=True
+        summand.astype(jnp.bfloat16), "row", scatter_dimension=1, tiled=True
     ).astype(jnp.float32)
 
 
@@ -35,19 +35,17 @@
     kv_lag = [kv]
     for i in range(1, kernel_len):
         kv_lag.append(jnp.where(row >= i, pltpu.roll(kv, i, 0), 0.0))
-    conv = jnp.zeros_like(kv)
-    for i in range(kernel_len):
+    conv = taps[0:1, :] * kv_lag[0]
+    for i in range(1, kernel_len):
         conv = conv + taps[i : i + 1, :] * kv_lag[i]
     gated_ref[...] = (q * conv).astype(gated_ref.dtype)
     gc = g * q
-    gp = jnp.zeros_like(gc)
+    gp = taps[0:1, :] * gc
     sums = []
     for i in range(kernel_len):
-        if i == 0:
-            lead = gc
-        else:
+        if i > 0:
             lead = jnp.where(row < tokens - i, pltpu.roll(gc, tokens - i, 0), 0.0)
-        gp = gp + taps[i : i + 1, :] * lead
+            gp = gp + taps[i : i + 1, :] * lead
         sums.append(jnp.sum(gc * kv_lag[i], axis=0, keepdims=True))
     sums.append(jnp.zeros((ts_ref.shape[0] - kernel_len, width), jnp.float32))
     ts_ref[...] = jnp.concatenate(sums, 0)
@@ -85,9 +83,9 @@
     col_width = inputs.shape[1]
     row_width = out_weight.shape[0]
     weight_flat = in_weight.reshape(col_width, 3 * row_width)
-    both_in = rows_in(jnp.concatenate([inputs, out_grad], axis=1))
-    whole_in = both_in[:, :col_width]
-    whole_grad = both_in[:, col_width:]
+    both_in = rows_in(jnp.stack([inputs, out_grad]))
+    whole_in = both_in[0]
+    whole_grad = both_in[1]
     all_tokens = whole_in.shape[0]
     grad_scale = 1.0 / math.sqrt(all_tokens)
 
@@ -129,9 +127,9 @@
     back_term = lax.dot_general(
         grad_flat, weight_flat, (((1,), (1,)), ((), ())), preferred_element_type=jnp.float32
     )
-    both_sums = fold_rows(jnp.concatenate([projected_term, back_term], axis=1))
-    projected = both_sums[:, :col_width]
-    back_sum = both_sums[:, col_width:]
+    both_sums = fold_rows(jnp.stack([projected_term, back_term]))
+    projected = both_sums[0]
+    back_sum = both_sums[1]
     result = (inputs.astype(jnp.float32) + projected).astype(jnp.bfloat16)
     input_grad = (out_grad.astype(jnp.float32) + back_sum).astype(jnp.bfloat16)
     return (result, input_grad, in_grad, out_w_grad, filter_grad)

time: 326 us -> 325 us (level)
  local copies, waits for them, and re-layouts: 14.1 us -> 10.1 us
    reduce_scatter x0 -> x1, waiting for transfers between devices: none -> 20.3 us  [fold_rows(): lax.psum_scatter(summand.astype(jnp.bfloat16), 'row', scatter_dimension=1...]
    unnamed x4 -> x3, waiting for transfers between devices: 20.1 us -> 0.05 us
    unnamed x26 -> x20, local copies, waits for them, and re-layouts: 12.3 us -> 8.31 us
where the time goes in v6:
time: 325 us; the launch traced here: 324 us
  waiting for transfers between devices  261 us (80%)
  matrix products  19.7 us (6%)
  Pallas kernels  13.9 us (4%)
  between operations  13.9 us (4%)
  local copies, waits for them, and re-layouts  10.1 us (3%)
  other arithmetic  5.7 us (2%)
    psum x1, waiting for transfers between devices, sum_cols(): return lax.psum(summand.astype(jnp.bfloat16), 'col')  212 us
    all_gather x1, waiting for transfers between devices, rows_in(): return lax.all_gather(operand, 'row', axis=1, tiled=True)  28.6 us
    reduce_scatter x1, waiting for transfers between devices, fold_rows(): lax.psum_scatter(summand.astype(jnp.bfloat16), 'row', scatter_dimension=1...  20.3 us
    pallas_call x1, Pallas kernels, gate_kernel(): pl.pallas_call(gate_body, grid=(tiles,), in_specs=[col(0), col(tiles), co...  13.9 us
    unnamed x20, local copies, waits for them, and re-layouts  8.31 us
  transfers between devices with their start and end apart: 3, of which 3 were waited for; matrix products, arithmetic and copies ran while one was open for 5% of the time, Pallas kernels for 0%

profile of v6, /device:TPU:2, one launch (start us, length us, event | category | flops | bytes accessed | tf_op | source)
XLA Modules:
  0.0 324.2 jit_solution(2381797001568141372)
XLA Ops:
  7.2 0.0 copy-start
  7.2 0.0 all-gather.2.cloned.1.call-start
  7.2 1.6 pad_maximum_fusion.1
  8.8 0.0 all-gather.2.cloned.1.call-update
  8.8 0.0 all-reduce.3.cloned.1.call-start
  8.9 1.7 copy.11
  10.6 28.6 %all-gather.2.cloned.1.call-done = bf16[2,1024,256]{2,1,0:T(8,128)(2,1)} async-done(((bf16[2,128,256]{2,1,0:T(8,128)(2,1)}), bf16[2,1024,256]{2,1,0:T(8,128)(2,1)}) %all-gather.2.cloned.1.call-update) | async-done | bytes 1048592 | tf_op jit(solution)/shard_map/all_gather | solution.py:12
  39.2 0.0 copy-done
  39.2 0.0 copy-start.2
  39.2 3.2 convolution_convert_fusion.1
  42.4 0.0 copy-done.2
  42.4 4.5 %convolution_convert_fusion = bf16[1024,3072]{1,0:T(8,128)(2,1)} fusion(bf16[256,3072]{0,1:T(8,128)(2,1)S(1)} %bitcast.41, bf16[2,1024,256]{2,1,0:T(8,128)(2,1)S(1)} %copy-done.2), kind=kOutput, calls=%fused_computation | convolution fusion | flops 1613758464 | bytes 8388608 | tf_op jit(solution)/shard_map/dot_general | solution.py:92
  46.9 0.0 all-reduce.3.cloned.1.call-update
  46.9 0.0 reduce-scatter.2.cloned.1.call-start
  46.9 211.8 %all-reduce.3.cloned.1.call-done = (bf16[1024,3072]{1,0:T(8,128)(2,1)}, bf16[1024,1024]{1,0:T(8,128)(2,1)}) async-done(((bf16[1024,3072]{1,0:T(8,128)(2,1)}, bf16[1024,1024]{1,0:T(8,128)(2,1)}), (bf16[1024,3072]{1,0:T(8,128)(2,1)}, bf16[1024,1024]{1,0:T(8,128)(2,1)})) %all-reduce.3.cloned.1.call-update) | async-done | bytes 8388624 | tf_op jit(solution)/shard_map/psum | solution.py:22
  258.8 13.9 %shard_map.92 = (bf16[1024,1024]{1,0:T(8,128)(2,1)}, bf16[1024,1024]{1,0:T(8,128)(2,1)}, bf16[1024,1024]{1,0:T(8,128)(2,1)}, bf16[1024,1024]{1,0:T(8,128)(2,1)}, f32[8,1024]{1,0:T(8,128)}) custom-call(bf16[1024,3072]{1,0:T(8,128)(2,1)} %get-tuple-element.25.q_ref.k_ref.v_ref, bf16[1024,3072]{1,0:T(8,128)(2,1)} %get-tuple-element.25.q_ref.k_ref.v_ref, ...), custom_call_target="tpu_custom_call" | custom-call | flops 62914560 | bytes 18874368 | tf_op jit(solution)/shard_map/pallas_call | solution.py:64
  272.7 0.0 copy-start.5
  272.7 2.4 fusion.2
  275.2 0.0 copy-done.5
  275.2 0.0 copy-start.4
  275.2 0.2 constant_dynamic-update-slice_fusion.2
  275.4 1.4 copy-done.4
  276.8 0.0 copy-start.3
  276.8 0.2 constant_dynamic-update-slice_fusion.1
  277.0 1.4 copy-done.3
  278.4 0.2 constant_dynamic-update-slice_fusion
  278.6 0.0 copy-start.1
  278.6 1.8 fusion.3
  280.4 0.8 copy-done.1
  281.2 1.2 pad_maximum_fusion
  282.4 0.0 reduce-scatter.2.cloned.1.call-update
  282.4 4.6 %fusion = bf16[256,3072]{1,0:T(8,128)(2,1)S(1)} fusion(bf16[1024,3072]{1,0:T(8,128)(2,1)} %copy-done.1, bf16[2,1024,256]{2,1,0:T(8,128)(2,1)S(1)} %copy-done.2), kind=kOutput, calls=%fused_computation.2 | convolution fusion | flops 1612185600 | bytes 8388608 | tf_op jit(solution)/shard_map/dot_general | solution.py:119
  287.0 1.6 copy.12
  288.6 2.6 copy.13
  291.2 1.4 multiply_bitcast_fusion
  292.5 0.0 copy-start.6
  292.6 0.0 copy-start.7
  292.6 3.2 fusion.1
  295.7 20.3 %reduce-scatter.2.cloned.1.call-done = bf16[2,128,256]{2,1,0:T(8,128)(2,1)} async-done(((bf16[2,1024,256]{2,1,0:T(8,128)(2,1)}), bf16[2,128,256]{2,1,0:T(8,128)(2,1)}) %reduce-scatter.2.cloned.1.call-update) | async-done | bytes 131088 | tf_op jit(solution)/shard_map/reduce_scatter | solution.py:16
  316.0 0.9 convert_element_type.31
  316.9 0.0 copy-done.6
  316.9 0.0 copy-done.7
  316.9 0.7 fusion.5
Async XLA Ops:
  7.2 32.0 %copy-start = (bf16[1024,256]{1,0:T(8,128)(2,1)S(1)}, bf16[1024,256]{1,0:T(8,128)(2,1)}, u32[]{:S(2)}) copy-start(bf16[1024,256]{1,0:T(8,128)(2,1)} %param.8) | copy-start | bytes 1572868
  7.2 32.0 %all-gather.2.cloned.1.call-start = ((), (), s32[]{:S(2)}) async-start(), calls=%async_computation.1 | async-start | bytes 1179648 | tf_op jit(solution)/shard_map/all_gather | solution.py:12
  8.8 249.9 %all-reduce.3.cloned.1.call-start = ((), (), s32[]{:S(2)}) async-start(), calls=%async_computation.3 | async-start | bytes 16777216 | tf_op jit(solution)/shard_map/psum | solution.py:22
  39.2 3.2 copy-start.2
  46.9 269.1 %reduce-scatter.2.cloned.1.call-start = ((), (), s32[]{:S(2)}) async-start(), calls=%async_computation.2 | async-start | bytes 1179648 | tf_op jit(solution)/shard_map/reduce_scatter | solution.py:16
  272.7 2.5 copy-start.5
  275.2 1.6 copy-start.4
  276.8 1.6 copy-start.3
  278.6 2.7 copy-start.1
  292.5 24.4 %copy-start.6 = (bf16[128,256]{1,0:T(8,128)(2,1)S(1)}, bf16[128,256]{1,0:T(8,128)(2,1)}, u32[]{:S(2)}) copy-start(bf16[128,256]{1,0:T(8,128)(2,1)} %param.6) | copy-start | bytes 196612
  292.6 24.4 %copy-start.7 = (bf16[128,256]{1,0:T(8,128)(2,1)S(1)}, bf16[128,256]{1,0:T(8,128)(2,1)}, u32[]{:S(2)}) copy-start(bf16[128,256]{1,0:T(8,128)(2,1)} %param.5) | copy-start | bytes 196612
Sparse Core Ops, SparseCore 0:
  10.4 28.7 all-gather.1
  47.0 211.7 all-reduce.2
  282.5 33.4 reduce-scatter.1

commit v7 on v6

--- a/solution.py
+++ b/solution.py
@@ -22,7 +22,7 @@
     return lax.psum(summand.astype(jnp.bfloat16), "col")
 
 
-def gate_body(q_ref, k_ref, v_ref, g_ref, t_ref, gated_ref, gq_ref, gk_ref, gv_ref, ts_ref):
+def gate_body(q_ref, k_ref, v_ref, g_ref, t_ref, gated_ref, gq_ref, gk_ref, gv_ref):
     tokens, width = q_ref.shape
     kernel_len = t_ref.shape[0]
     q = q_ref[...].astype(jnp.float32)
@@ -32,26 +32,36 @@
     taps = t_ref[...]
     row = lax.broadcasted_iota(jnp.int32, (tokens, width), 0)
     kv = k * v
-    kv_lag = [kv]
+    conv = taps[0:1, :] * kv
     for i in range(1, kernel_len):
-        kv_lag.append(jnp.where(row >= i, pltpu.roll(kv, i, 0), 0.0))
-    conv = taps[0:1, :] * kv_lag[0]
-    for i in range(1, kernel_len):
-        conv = conv + taps[i : i + 1, :] * kv_lag[i]
+        conv = conv + taps[i : i + 1, :] * jnp.where(row >= i, pltpu.roll(kv, i, 0), 0.0)
     gated_ref[...] = (q * conv).astype(gated_ref.dtype)
     gc = g * q
     gp = taps[0:1, :] * gc
-    sums = []
-    for i in range(kernel_len):
-        if i > 0:
-            lead = jnp.where(row < tokens - i, pltpu.roll(gc, tokens - i, 0), 0.0)
-            gp = gp + taps[i : i + 1, :] * lead
-        sums.append(jnp.sum(gc * kv_lag[i], axis=0, keepdims=True))
-    sums.append(jnp.zeros((ts_ref.shape[0] - kernel_len, width), jnp.float32))
-    ts_ref[...] = jnp.concatenate(sums, 0)
+    for i in range(1, kernel_len):
+        lead = jnp.where(row < tokens - i, pltpu.roll(gc, tokens - i, 0), 0.0)
+        gp = gp + taps[i : i + 1, :] * lead
     gq_ref[...] = (g * conv).astype(gq_ref.dtype)
     gk_ref[...] = (gp * v).astype(gk_ref.dtype)
     gv_ref[...] = (gp * k).astype(gv_ref.dtype)
+
+
+def tap_body(q_ref, k_ref, v_ref, g_ref, ts_ref):
+    tokens, width = q_ref.shape
+    kernel_len = ts_ref.shape[0] - 1
+    q = q_ref[...].astype(jnp.float32)
+    k = k_ref[...].astype(jnp.float32)
+    v = v_ref[...].astype(jnp.float32)
+    g = g_ref[...].astype(jnp.float32)
+    row = lax.broadcasted_iota(jnp.int32, (tokens, width), 0)
+    kv = k * v
+    gc = g * q
+    sums = [jnp.sum(gc * kv, axis=0, keepdims=True)]
+    for i in range(1, kernel_len):
+        lagged = jnp.where(row >= i, pltpu.roll(kv, i, 0), 0.0)
+        sums.append(jnp.sum(gc * lagged, axis=0, keepdims=True))
+    sums.append(jnp.zeros((ts_ref.shape[0] - kernel_len, width), jnp.float32))
+    ts_ref[...] = jnp.concatenate(sums, 0)
 
 
 def gate_kernel(mixed_flat, grad_gated, taps_t, width=128):
@@ -61,7 +71,8 @@
     tiles = channels // width
     col = lambda off: pl.BlockSpec((tokens, width), lambda j: (0, j + off))
     half = jax.ShapeDtypeStruct((tokens, channels), jnp.bfloat16)
-    return pl.pallas_call(
+    operands = (mixed_flat, mixed_flat, mixed_flat, grad_gated)
+    gated, grad_query, grad_key, grad_value = pl.pallas_call(
         gate_body,
         grid=(tiles,),
         in_specs=[
@@ -71,12 +82,23 @@
             col(0),
             pl.BlockSpec((kernel_len, width), lambda j: (0, j)),
         ],
-        out_specs=[col(0), col(0), col(0), col(0), pl.BlockSpec((8, width), lambda j: (0, j))],
-        out_shape=[half, half, half, half, jax.ShapeDtypeStruct((8, channels), jnp.float32)],
+        out_specs=[col(0), col(0), col(0), col(0)],
+        out_shape=[half, half, half, half],
         cost_estimate=pl.CostEstimate(
-            flops=60 * tokens * channels, transcendentals=0, bytes_accessed=18 * tokens * channels
+            flops=45 * tokens * channels, transcendentals=0, bytes_accessed=16 * tokens * channels
         ),
-    )(mixed_flat, mixed_flat, mixed_flat, grad_gated, taps_t)
+    )(*operands, taps_t)
+    tap_sums = pl.pallas_call(
+        tap_body,
+        grid=(tiles,),
+        in_specs=[col(0), col(tiles), col(2 * tiles), col(0)],
+        out_specs=pl.BlockSpec((kernel_len + 1, width), lambda j: (0, j)),
+        out_shape=jax.ShapeDtypeStruct((kernel_len + 1, channels), jnp.float32),
+        cost_estimate=pl.CostEstimate(
+            flops=30 * tokens * channels, transcendentals=0, bytes_accessed=8 * tokens * channels
+        ),
+    )(*operands)
+    return gated, grad_query, grad_key, grad_value, tap_sums
 
 
 def on_device(inputs, out_grad, in_weight, out_weight, filter_taps):

time: 325 us -> 323 us (level)
  waiting for transfers between devices: 261 us -> 252 us
  Pallas kernels: 13.9 us -> 21.5 us
    pallas_call x0 -> x1, Pallas kernels: none -> 9.25 us  [gate_kernel(): pl.pallas_call(tap_body, grid=(tiles,), in_specs=[col(0), col(tiles), col...]
    reduce_scatter x1, waiting for transfers between devices: 20.3 us -> 11.1 us  [fold_rows(): lax.psum_scatter(summand.astype(jnp.bfloat16), 'row', scatter_dimension=1...]
  transfers between devices with their start and end apart: 3 -> 3, of which waited for: 3 -> 3; matrix products, arithmetic and copies ran while one was open for 5% -> 5% of each run, Pallas kernels for 0% -> 3%
where the time goes in v7:
time: 323 us; the launch traced here: 322 us
  waiting for transfers between devices  252 us (78%)
  Pallas kernels  21.5 us (7%)
  matrix products  19.7 us (6%)
  between operations  13.8 us (4%)
  local copies, waits for them, and re-layouts  10 us (3%)
  other arithmetic  5.62 us (2%)
    psum x1, waiting for transfers between devices, sum_cols(): return lax.psum(summand.astype(jnp.bfloat16), 'col')  212 us
    all_gather x1, waiting for transfers between devices, rows_in(): return lax.all_gather(operand, 'row', axis=1, tiled=True)  28.6 us
    pallas_call x1, Pallas kernels, gate_kernel(): pl.pallas_call(gate_body, grid=(tiles,), in_specs=[col(0), col(tiles), co...  12.2 us
    reduce_scatter x1, waiting for transfers between devices, fold_rows(): lax.psum_scatter(summand.astype(jnp.bfloat16), 'row', scatter_dimension=1...  11.1 us
    pallas_call x1, Pallas kernels, gate_kernel(): pl.pallas_call(tap_body, grid=(tiles,), in_specs=[col(0), col(tiles), col...  9.25 us
    unnamed x20, local copies, waits for them, and re-layouts  8.3 us
  transfers between devices with their start and end apart: 3, of which 3 were waited for; matrix products, arithmetic and copies ran while one was open for 5% of the time, Pallas kernels for 3%

profile of v7, /device:TPU:2, one launch (start us, length us, event | category | flops | bytes accessed | tf_op | source)
XLA Modules:
  0.0 322.4 jit_solution(17052030411783224837)
XLA Ops:
  7.2 0.0 copy-start
  7.2 0.0 all-gather.2.cloned.1.call-start
  7.2 1.6 pad_maximum_fusion.1
  8.8 0.0 all-gather.2.cloned.1.call-update
  8.8 0.0 all-reduce.3.cloned.1.call-start
  8.9 1.7 copy.11
  10.6 28.6 %all-gather.2.cloned.1.call-done = bf16[2,1024,256]{2,1,0:T(8,128)(2,1)} async-done(((bf16[2,128,256]{2,1,0:T(8,128)(2,1)}), bf16[2,1024,256]{2,1,0:T(8,128)(2,1)}) %all-gather.2.cloned.1.call-update) | async-done | bytes 1048592 | tf_op jit(solution)/shard_map/all_gather | solution.py:12
  39.2 0.0 copy-done
  39.2 0.0 copy-start.2
  39.2 3.2 convolution_convert_fusion.1
  42.4 0.0 copy-done.2
  42.4 4.5 %convolution_convert_fusion = bf16[1024,3072]{1,0:T(8,128)(2,1)} fusion(bf16[256,3072]{0,1:T(8,128)(2,1)S(1)} %bitcast.41, bf16[2,1024,256]{2,1,0:T(8,128)(2,1)S(1)} %copy-done.2), kind=kOutput, calls=%fused_computation | convolution fusion | flops 1613758464 | bytes 8388608 | tf_op jit(solution)/shard_map/dot_general | solution.py:114
  46.9 0.0 all-reduce.3.cloned.1.call-update
  46.9 0.0 reduce-scatter.2.cloned.1.call-start
  46.9 211.8 %all-reduce.3.cloned.1.call-done = (bf16[1024,3072]{1,0:T(8,128)(2,1)}, bf16[1024,1024]{1,0:T(8,128)(2,1)}) async-done(((bf16[1024,3072]{1,0:T(8,128)(2,1)}, bf16[1024,1024]{1,0:T(8,128)(2,1)}), (bf16[1024,3072]{1,0:T(8,128)(2,1)}, bf16[1024,1024]{1,0:T(8,128)(2,1)})) %all-reduce.3.cloned.1.call-update) | async-done | bytes 8388624 | tf_op jit(solution)/shard_map/psum | solution.py:22
  258.8 12.2 %shard_map.92 = (bf16[1024,1024]{1,0:T(8,128)(2,1)}, bf16[1024,1024]{1,0:T(8,128)(2,1)}, bf16[1024,1024]{1,0:T(8,128)(2,1)}, bf16[1024,1024]{1,0:T(8,128)(2,1)}) custom-call(bf16[1024,3072]{1,0:T(8,128)(2,1)} %get-tuple-element.23.q_ref.k_ref.v_ref, bf16[1024,3072]{1,0:T(8,128)(2,1)} %get-tuple-element.23.q_ref.k_ref.v_ref, ...), custom_call_target="tpu_custom_call" | custom-call | flops 47185920 | bytes 16777216 | tf_op jit(solution)/shard_map/pallas_call | solution.py:75
  271.0 0.0 copy-start.5
  271.0 2.4 fusion.2
  273.5 0.0 copy-done.5
  273.5 0.0 copy-start.4
  273.5 0.2 constant_dynamic-update-slice_fusion.2
  273.7 1.4 copy-done.4
  275.1 0.0 copy-start.3
  275.1 0.2 constant_dynamic-update-slice_fusion.1
  275.2 1.4 copy-done.3
  276.6 0.2 constant_dynamic-update-slice_fusion
  276.8 0.0 copy-start.1
  276.8 1.8 fusion.3
  278.6 0.8 copy-done.1
  279.5 1.1 pad_maximum_fusion
  280.5 0.0 reduce-scatter.2.cloned.1.call-update
  280.6 4.6 %fusion = bf16[256,3072]{1,0:T(8,128)(2,1)S(1)} fusion(bf16[1024,3072]{1,0:T(8,128)(2,1)} %copy-done.1, bf16[2,1024,256]{2,1,0:T(8,128)(2,1)S(1)} %copy-done.2), kind=kOutput, calls=%fused_computation.2 | convolution fusion | flops 1612185600 | bytes 8388608 | tf_op jit(solution)/shard_map/dot_general | solution.py:141
  285.2 1.6 copy.12
  286.7 2.6 copy.13
  289.3 9.3 %shard_map.93 = f32[8,1024]{1,0:T(8,128)} custom-call(bf16[1024,3072]{1,0:T(8,128)(2,1)} %get-tuple-element.23.q_ref.k_ref.v_ref, bf16[1024,3072]{1,0:T(8,128)(2,1)} %get-tuple-element.23.q_ref.k_ref.v_ref, bf16[1024,3072]{1,0:T(8,128)(2,1)} %get-tuple-element.23.q_ref.k_ref.v_ref, bf16[1024,1024]{1,0:T(8,128)(2,1)} %get-tuple-element.24.g_ref), custom_call_target="tpu_custom_call" | custom-call | flops 31457280 | bytes 8388608 | tf_op jit(solution)/shard_map/pallas_call | solution.py:91
  298.6 1.4 multiply_bitcast_fusion
  299.9 0.0 copy-start.6
  299.9 0.0 copy-start.7
  299.9 3.2 fusion.1
  303.1 11.1 %reduce-scatter.2.cloned.1.call-done = bf16[2,128,256]{2,1,0:T(8,128)(2,1)} async-done(((bf16[2,1024,256]{2,1,0:T(8,128)(2,1)}), bf16[2,128,256]{2,1,0:T(8,128)(2,1)}) %reduce-scatter.2.cloned.1.call-update) | async-done | bytes 131088 | tf_op jit(solution)/shard_map/reduce_scatter | solution.py:16
  314.3 0.9 convert_element_type.31
  315.2 0.0 copy-done.6
  315.2 0.0 copy-done.7
  315.2 0.7 fusion.5
Async XLA Ops:
  7.2 32.0 %copy-start = (bf16[1024,256]{1,0:T(8,128)(2,1)S(1)}, bf16[1024,256]{1,0:T(8,128)(2,1)}, u32[]{:S(2)}) copy-start(bf16[1024,256]{1,0:T(8,128)(2,1)} %param.8) | copy-start | bytes 1572868
  7.2 32.0 %all-gather.2.cloned.1.call-start = ((), (), s32[]{:S(2)}) async-start(), calls=%async_computation.1 | async-start | bytes 1179648 | tf_op jit(solution)/shard_map/all_gather | solution.py:12
  8.8 249.9 %all-reduce.3.cloned.1.call-start = ((), (), s32[]{:S(2)}) async-start(), calls=%async_computation.3 | async-start | bytes 16777216 | tf_op jit(solution)/shard_map/psum | solution.py:22
  39.2 3.2 copy-start.2
  46.9 267.4 %reduce-scatter.2.cloned.1.call-start = ((), (), s32[]{:S(2)}) async-start(), calls=%async_computation.2 | async-start | bytes 1179648 | tf_op jit(solution)/shard_map/reduce_scatter | solution.py:16
  271.0 2.5 copy-start.5
  273.5 1.6 copy-start.4
  275.1 1.6 copy-start.3
  276.8 2.6 copy-start.1
  299.9 15.3 %copy-start.6 = (bf16[128,256]{1,0:T(8,128)(2,1)S(1)}, bf16[128,256]{1,0:T(8,128)(2,1)}, u32[]{:S(2)}) copy-start(bf16[128,256]{1,0:T(8,128)(2,1)} %param.6) | copy-start | bytes 196612
  299.9 15.3 %copy-start.7 = (bf16[128,256]{1,0:T(8,128)(2,1)S(1)}, bf16[128,256]{1,0:T(8,128)(2,1)}, u32[]{:S(2)}) copy-start(bf16[128,256]{1,0:T(8,128)(2,1)} %param.5) | copy-start | bytes 196612
Sparse Core Ops, SparseCore 0:
  10.4 28.7 all-gather.1
  47.0 211.7 all-reduce.2
  280.7 33.5 reduce-scatter.1

commit v8 on v7

--- a/solution.py
+++ b/solution.py
@@ -13,9 +13,16 @@
 
 
 def fold_rows(summand):
-    return lax.psum_scatter(
-        summand.astype(jnp.bfloat16), "row", scatter_dimension=1, tiled=True
-    ).astype(jnp.float32)
+    devices = lax.axis_size("row")
+    me = lax.axis_index("row")
+    lead, rows = summand.shape[0], summand.shape[1] // devices
+    parts = summand.astype(jnp.bfloat16).reshape((lead, devices, rows) + summand.shape[2:])
+    total = lax.dynamic_index_in_dim(parts, me, 1, keepdims=False).astype(jnp.float32)
+    for dist in range(1, devices):
+        pairs = [(i, (i + dist) % devices) for i in range(devices)]
+        block = lax.dynamic_index_in_dim(parts, (me + dist) % devices, 1, keepdims=False)
+        total = total + lax.ppermute(block, "row", pairs).astype(jnp.float32)
+    return total
 
 
 def sum_cols(summand):

time: 323 us -> 318 us (0.985)
  waiting for transfers between devices: 252 us -> 240 us
  starting transfers between devices: 0.12 us -> 9.29 us
  matrix products: 19.7 us -> 15.3 us
    reduce_scatter x1 -> x0, waiting for transfers between devices: 11.1 us -> none  [fold_rows(): lax.psum_scatter(summand.astype(jnp.bfloat16), 'row', scatter_dimension=1...]
    ppermute x0 -> x7, starting transfers between devices: none -> 9.21 us  [fold_rows(): total = total + lax.ppermute(block, 'row', pairs).astype(jnp.float32)]
    unnamed x20 -> x28, local copies, waits for them, and re-layouts: 8.3 us -> 7.68 us
  transfers between devices with their start and end apart: 3 -> 9, of which waited for: 3 -> 2; matrix products, arithmetic and copies ran while one was open for 5% -> 4% of each run, Pallas kernels for 3% -> 3%
where the time goes in v8:
time: 318 us; the launch traced here: 316 us
  waiting for transfers between devices  240 us (75%)
  Pallas kernels  21.5 us (7%)
  matrix products  15.3 us (5%)
  between operations  14.3 us (4%)
  local copies, waits for them, and re-layouts  9.41 us (3%)
  starting transfers between devices  9.29 us (3%)
  other arithmetic  5.81 us (2%)
    psum x1, waiting for transfers between devices, sum_cols(): return lax.psum(summand.astype(jnp.bfloat16), 'col')  212 us
    all_gather x1, waiting for transfers between devices, rows_in(): return lax.all_gather(operand, 'row', axis=1, tiled=True)  28.6 us
    pallas_call x1, Pallas kernels, gate_kernel(): pl.pallas_call(gate_body, grid=(tiles,), in_specs=[col(0), col(tiles), co...  12.2 us
    pallas_call x1, Pallas kernels, gate_kernel(): pl.pallas_call(tap_body, grid=(tiles,), in_specs=[col(0), col(tiles), col...  9.34 us
    ppermute x7, starting transfers between devices, fold_rows(): total = total + lax.ppermute(block, 'row', pairs).astype(jnp.float32)  9.21 us
    unnamed x28, local copies, waits for them, and re-layouts  7.68 us
  transfers between devices with their start and end apart: 9, of which 2 were waited for; matrix products, arithmetic and copies ran while one was open for 4% of the time, Pallas kernels for 3%

profile of v8, /device:TPU:2, one launch (start us, length us, event | category | flops | bytes accessed | tf_op | source)
XLA Modules:
  0.0 316.1 jit_solution(14362996208974329504)
XLA Ops:
  7.2 0.0 copy-start
  7.2 0.0 all-gather.2.cloned.1.call-start
  7.2 1.6 pad_maximum_fusion
  8.8 0.0 all-gather.2.cloned.1.call-update
  8.8 0.0 all-reduce.3.cloned.1.call-start
  8.9 1.7 copy.11
  10.6 28.6 %all-gather.2.cloned.1.call-done = bf16[2,1024,256]{2,1,0:T(8,128)(2,1)} async-done(((bf16[2,128,256]{2,1,0:T(8,128)(2,1)}), bf16[2,1024,256]{2,1,0:T(8,128)(2,1)}) %all-gather.2.cloned.1.call-update) | async-done | bytes 1048592 | tf_op jit(solution)/shard_map/all_gather | solution.py:12
  39.2 0.0 copy-done
  39.2 0.0 copy-start.1
  39.2 3.2 %convolution_convert_fusion.1 = bf16[1024,1024]{1,0:T(8,128)(2,1)} fusion(bf16[1024,256]{1,0:T(8,128)(2,1)S(1)} %copy-done, bf16[2,1024,256]{2,1,0:T(8,128)(2,1)} %all-gather.2.cloned.1.call-done), kind=kOutput, calls=%fused_computation.19 | convolution fusion | flops 537919488 | bytes 3145728 | tf_op jit(solution)/shard_map/dot_general | solution.py:122
  42.4 0.0 copy-done.1
  42.4 4.4 %convolution_convert_fusion = bf16[1024,3072]{1,0:T(8,128)(2,1)} fusion(bf16[256,3072]{0,1:T(8,128)(2,1)S(1)} %bitcast.61, bf16[2,1024,256]{2,1,0:T(8,128)(2,1)S(1)} %copy-done.1), kind=kOutput, calls=%fused_computation | convolution fusion | flops 1613758464 | bytes 8388608 | tf_op jit(solution)/shard_map/dot_general | solution.py:121
  46.8 0.0 all-reduce.3.cloned.1.call-update
  47.0 211.8 %all-reduce.3.cloned.1.call-done = (bf16[1024,3072]{1,0:T(8,128)(2,1)}, bf16[1024,1024]{1,0:T(8,128)(2,1)}) async-done(((bf16[1024,3072]{1,0:T(8,128)(2,1)}, bf16[1024,1024]{1,0:T(8,128)(2,1)}), (bf16[1024,3072]{1,0:T(8,128)(2,1)}, bf16[1024,1024]{1,0:T(8,128)(2,1)})) %all-reduce.3.cloned.1.call-update) | async-done | bytes 8388624 | tf_op jit(solution)/shard_map/psum | solution.py:29
  258.8 12.2 %shard_map.92 = (bf16[1024,1024]{1,0:T(8,128)(2,1)}, bf16[1024,1024]{1,0:T(8,128)(2,1)}, bf16[1024,1024]{1,0:T(8,128)(2,1)}, bf16[1024,1024]{1,0:T(8,128)(2,1)}) custom-call(bf16[1024,3072]{1,0:T(8,128)(2,1)} %get-tuple-element.23.q_ref.k_ref.v_ref, bf16[1024,3072]{1,0:T(8,128)(2,1)} %get-tuple-element.23.q_ref.k_ref.v_ref, ...), custom_call_target="tpu_custom_call" | custom-call | flops 47185920 | bytes 16777216 | tf_op jit(solution)/shard_map/pallas_call | solution.py:82
  271.0 0.0 copy-start.8
  271.0 2.4 convolution_convert_fusion.3
  273.5 0.0 copy-start.2
  273.5 0.0 copy-done.8
  273.5 0.0 copy-start.7
  273.5 0.2 constant_dynamic-update-slice_fusion.2
  273.7 1.6 copy-done.7
  275.3 0.0 copy-start.6
  275.3 0.2 constant_dynamic-update-slice_fusion.1
  275.4 1.4 copy-done.6
  276.8 0.2 constant_dynamic-update-slice_fusion
  277.0 1.8 fusion.2
  278.8 0.0 copy-start.4
  278.9 2.0 collective-permute-start.6
  280.9 0.0 copy-done.2
  280.9 0.9 fusion.26
  281.8 0.0 collective-permute-start
  281.8 0.0 collective-permute-start.1
  281.8 1.7 collective-permute-start.2
  283.5 0.0 copy-done.4
  283.5 0.0 copy-start.11
  283.5 2.7 collective-permute-start.3
  286.2 1.9 fusion
  288.1 0.0 collective-permute-done.6
  288.1 1.3 collective-permute-start.4
  289.4 0.0 collective-permute-done
  289.4 1.4 collective-permute-start.5
  290.9 0.0 copy-done.11
  290.9 1.6 fusion.1
  292.4 1.6 copy.13
  294.0 2.6 copy.14
  296.6 0.0 copy-start.3
  296.6 0.0 copy-start.5
  296.6 9.3 %shard_map.93 = f32[8,1024]{1,0:T(8,128)} custom-call(bf16[1024,3072]{1,0:T(8,128)(2,1)} %get-tuple-element.23.q_ref.k_ref.v_ref, bf16[1024,3072]{1,0:T(8,128)(2,1)} %get-tuple-element.23.q_ref.k_ref.v_ref, bf16[1024,3072]{1,0:T(8,128)(2,1)} %get-tuple-element.23.q_ref.k_ref.v_ref, bf16[1024,1024]{1,0:T(8,128)(2,1)} %get-tuple-element.24.g_ref), custom_call_target="tpu_custom_call" | custom-call | flops 31457280 | bytes 8388608 | tf_op jit(solution)/shard_map/pallas_call | solution.py:98
  305.9 0.0 copy-start.9
  305.9 0.0 copy-start.10
  305.9 1.4 fusion.29
  307.3 0.0 collective-permute-done.1
  307.3 0.0 collective-permute-done.2
  307.3 0.0 collective-permute-done.3
  307.3 0.0 collective-permute-done.4
  307.3 0.0 collective-permute-done.5
  307.4 0.0 copy-done.3
  307.4 0.0 copy-done.5
  307.4 1.2 fusion.8
  308.6 0.0 copy-done.9
  308.6 0.0 copy-done.10
  308.6 0.7 fusion.18
  (1 shorter events, 0.0 us)
Async XLA Ops:
  7.2 32.0 %copy-start = (bf16[1024,256]{1,0:T(8,128)(2,1)S(1)}, bf16[1024,256]{1,0:T(8,128)(2,1)}, u32[]{:S(2)}) copy-start(bf16[1024,256]{1,0:T(8,128)(2,1)} %param.8) | copy-start | bytes 1572868
  7.2 32.0 %all-gather.2.cloned.1.call-start = ((), (), s32[]{:S(2)}) async-start(), calls=%async_computation | async-start | bytes 1179648 | tf_op jit(solution)/shard_map/all_gather | solution.py:12
  8.8 249.9 %all-reduce.3.cloned.1.call-start = ((), (), s32[]{:S(2)}) async-start(), calls=%async_computation.1 | async-start | bytes 16777216 | tf_op jit(solution)/shard_map/psum | solution.py:29
  39.2 3.2 %copy-start.1 = (bf16[2,1024,256]{2,1,0:T(8,128)(2,1)S(1)}, bf16[2,1024,256]{2,1,0:T(8,128)(2,1)}, u32[]{:S(2)}) copy-start(bf16[2,1024,256]{2,1,0:T(8,128)(2,1)} %all-gather.2.cloned.1.call-done) | copy-start | bytes 3145732
  271.0 2.5 copy-start.8
  273.5 7.4 %copy-start.2 = (bf16[1024,256]{1,0:T(8,128)(2,1)}, bf16[1024,256]{1,0:T(8,128)(2,1)S(1)}, u32[]{:S(2)}) copy-start(bf16[1024,256]{1,0:T(8,128)(2,1)S(1)} %convolution_convert_fusion.3) | copy-start | bytes 1572868
  273.5 1.8 copy-start.7
  275.3 1.6 copy-start.6
  278.8 4.7 %copy-start.4 = (bf16[1,8,128,256]{3,2,1,0:T(8,128)(2,1)}, bf16[1,8,128,256]{3,2,1,0:T(8,128)(2,1)S(1)}, u32[]{:S(2)}) copy-start(bf16[1,8,128,256]{3,2,1,0:T(8,128)(2,1)S(1)} %fusion.2) | copy-start | bytes 1572868
  278.9 9.2 %collective-permute-start.6 = (bf16[2,128,256]{2,1,0:T(8,128)(2,1)S(1)}, bf16[2,128,256]{2,1,0:T(8,128)(2,1)S(1)}, u32[]{:S(2)}, u32[]{:S(2)}) collective-permute-start(bf16[2,128,256]{2,1,0:T(8,128)(2,1)S(1)} %fusion.27), channel_id=1, source_target_pairs={{0,224},{32,0},{64,32},{96,64},{128,96},{160,128},{192,160},{224,1... | collective-permute-start | bytes 393224 | tf_op jit(solution)/shard_map/ppermute | solution.py:24
  281.8 7.7 %collective-permute-start = (bf16[2,128,256]{2,1,0:T(8,128)(2,1)S(1)}, bf16[2,128,256]{2,1,0:T(8,128)(2,1)S(1)}, u32[]{:S(2)}, u32[]{:S(2)}) collective-permute-start(bf16[2,128,256]{2,1,0:T(8,128)(2,1)S(1)} %get-tuple-element.25), channel_id=1, source_target_pairs={{0,32},{32,64},{64,96},{96,128},{128,160},{160,192},{192,224},{224... | collective-permute-start | bytes 393224 | tf_op jit(solution)/shard_map/ppermute | solution.py:24
  281.8 25.5 %collective-permute-start.1 = (bf16[2,128,256]{2,1,0:T(8,128)(2,1)}, bf16[2,128,256]{2,1,0:T(8,128)(2,1)S(1)}, u32[]{:S(2)}, u32[]{:S(2)}) collective-permute-start(bf16[2,128,256]{2,1,0:T(8,128)(2,1)} %get-tuple-element.26), channel_id=1, source_target_pairs={{0,64},{32,96},{64,128},{96,160},{128,192},{160,224},{192,0},{224,... | collective-permute-start | bytes 393224 | tf_op jit(solution)/shard_map/ppermute | solution.py:24
  281.8 25.5 %collective-permute-start.2 = (bf16[2,128,256]{2,1,0:T(8,128)(2,1)}, bf16[2,128,256]{2,1,0:T(8,128)(2,1)}, u32[]{:S(2)}, u32[]{:S(2)}) collective-permute-start(bf16[2,128,256]{2,1,0:T(8,128)(2,1)} %get-tuple-element.27), channel_id=1, source_target_pairs={{0,96},{32,128},{64,160},{96,192},{128,224},{160,0},{192,32},{224,... | collective-permute-start | bytes 393224 | tf_op jit(solution)/shard_map/ppermute | solution.py:24
  283.5 7.4 %copy-start.11 = (bf16[1024,1024]{1,0:T(8,128)(2,1)S(1)}, bf16[1024,1024]{1,0:T(8,128)(2,1)}, u32[]{:S(2)}) copy-start(bf16[1024,1024]{1,0:T(8,128)(2,1)} %get-tuple-element.9) | copy-start | bytes 6291460
  283.5 23.9 %collective-permute-start.3 = (bf16[2,128,256]{2,1,0:T(8,128)(2,1)}, bf16[2,128,256]{2,1,0:T(8,128)(2,1)}, u32[]{:S(2)}, u32[]{:S(2)}) collective-permute-start(bf16[2,128,256]{2,1,0:T(8,128)(2,1)} %get-tuple-element.28), channel_id=1, source_target_pairs={{0,128},{32,160},{64,192},{96,224},{128,0},{160,32},{192,64},{224,... | collective-permute-start | bytes 393224 | tf_op jit(solution)/shard_map/ppermute | solution.py:24
  288.1 19.2 %collective-permute-start.4 = (bf16[2,128,256]{2,1,0:T(8,128)(2,1)}, bf16[2,128,256]{2,1,0:T(8,128)(2,1)}, u32[]{:S(2)}, u32[]{:S(2)}) collective-permute-start(bf16[2,128,256]{2,1,0:T(8,128)(2,1)} %get-tuple-element.29), channel_id=1, source_target_pairs={{0,160},{32,192},{64,224},{96,0},{128,32},{160,64},{192,96},{224,1... | collective-permute-start | bytes 393224 | tf_op jit(solution)/shard_map/ppermute | solution.py:24
  289.4 17.9 %collective-permute-start.5 = (bf16[2,128,256]{2,1,0:T(8,128)(2,1)}, bf16[2,128,256]{2,1,0:T(8,128)(2,1)}, u32[]{:S(2)}, u32[]{:S(2)}) collective-permute-start(bf16[2,128,256]{2,1,0:T(8,128)(2,1)} %get-tuple-element.30), channel_id=1, source_target_pairs={{0,192},{32,224},{64,0},{96,32},{128,64},{160,96},{192,128},{224,1... | collective-permute-start | bytes 393224 | tf_op jit(solution)/shard_map/ppermute | solution.py:24
  296.6 10.8 %copy-start.3 = (bf16[1024,256]{1,0:T(8,128)(2,1)S(1)}, bf16[1024,256]{1,0:T(8,128)(2,1)}, u32[]{:S(2)}) copy-start(bf16[1024,256]{1,0:T(8,128)(2,1)} %copy-done.2) | copy-start | bytes 1572868
  296.6 10.8 %copy-start.5 = (bf16[1,8,128,256]{3,2,1,0:T(8,128)(2,1)S(1)}, bf16[1,8,128,256]{3,2,1,0:T(8,128)(2,1)}, u32[]{:S(2)}) copy-start(bf16[1,8,128,256]{3,2,1,0:T(8,128)(2,1)} %copy-done.4) | copy-start | bytes 1572868
  305.9 2.7 copy-start.9
  305.9 2.7 copy-start.10
Sparse Core Ops, SparseCore 0:
  10.4 28.7 all-gather.1
  47.0 211.7 all-reduce.2

commit v9 on v6

--- a/solution.py
+++ b/solution.py
@@ -13,9 +13,16 @@
 
 
 def fold_rows(summand):
-    return lax.psum_scatter(
-        summand.astype(jnp.bfloat16), "row", scatter_dimension=1, tiled=True
-    ).astype(jnp.float32)
+    devices = lax.axis_size("row")
+    me = lax.axis_index("row")
+    lead, rows = summand.shape[0], summand.shape[1] // devices
+    parts = summand.astype(jnp.bfloat16).reshape((lead, devices, rows) + summand.shape[2:])
+    total = lax.dynamic_index_in_dim(parts, me, 1, keepdims=False).astype(jnp.float32)
+    for dist in range(1, devices):
+        pairs = [(i, (i + dist) % devices) for i in range(devices)]
+        block = lax.dynamic_index_in_dim(parts, (me + dist) % devices, 1, keepdims=False)
+        total = total + lax.ppermute(block, "row", pairs).astype(jnp.float32)
+    return total
 
 
 def sum_cols(summand):

time: 325 us -> 310 us (0.954)
  waiting for transfers between devices: 261 us -> 240 us
  starting transfers between devices: 0.12 us -> 9.29 us
  matrix products: 19.7 us -> 15.3 us
    reduce_scatter x1 -> x0, waiting for transfers between devices: 20.3 us -> none  [fold_rows(): lax.psum_scatter(summand.astype(jnp.bfloat16), 'row', scatter_dimension=1...]
    ppermute x0 -> x7, starting transfers between devices: none -> 9.21 us  [fold_rows(): total = total + lax.ppermute(block, 'row', pairs).astype(jnp.float32)]
    unnamed x20 -> x28, local copies, waits for them, and re-layouts: 8.31 us -> 7.78 us
  transfers between devices with their start and end apart: 3 -> 9, of which waited for: 3 -> 2; matrix products, arithmetic and copies ran while one was open for 5% -> 4% of each run, Pallas kernels for 0% -> 0%
where the time goes in v9:
time: 310 us; the launch traced here: 309 us
  waiting for transfers between devices  240 us (77%)
  matrix products  15.3 us (5%)
  between operations  14.3 us (5%)
  Pallas kernels  13.9 us (4%)
  local copies, waits for them, and re-layouts  9.56 us (3%)
  starting transfers between devices  9.29 us (3%)
  other arithmetic  5.72 us (2%)
    psum x1, waiting for transfers between devices, sum_cols(): return lax.psum(summand.astype(jnp.bfloat16), 'col')  212 us
    all_gather x1, waiting for transfers between devices, rows_in(): return lax.all_gather(operand, 'row', axis=1, tiled=True)  28.6 us
    pallas_call x1, Pallas kernels, gate_kernel(): pl.pallas_call(gate_body, grid=(tiles,), in_specs=[col(0), col(tiles), co...  13.9 us
    ppermute x7, starting transfers between devices, fold_rows(): total = total + lax.ppermute(block, 'row', pairs).astype(jnp.float32)  9.21 us
    unnamed x28, local copies, waits for them, and re-layouts  7.78 us
  transfers between devices with their start and end apart: 9, of which 2 were waited for; matrix products, arithmetic and copies ran while one was open for 4% of the time, Pallas kernels for 0%

profile of v9, /device:TPU:2, one launch (start us, length us, event | category | flops | bytes accessed | tf_op | source)
XLA Modules:
  0.0 308.6 jit_solution(4702321536484821509)
XLA Ops:
  7.2 0.0 copy-start
  7.2 0.0 all-gather.2.cloned.1.call-start
  7.2 1.6 pad_maximum_fusion
  8.8 0.0 all-gather.2.cloned.1.call-update
  8.8 0.0 all-reduce.3.cloned.1.call-start
  8.9 1.7 copy.11
  10.6 28.6 %all-gather.2.cloned.1.call-done = bf16[2,1024,256]{2,1,0:T(8,128)(2,1)} async-done(((bf16[2,128,256]{2,1,0:T(8,128)(2,1)}), bf16[2,1024,256]{2,1,0:T(8,128)(2,1)}) %all-gather.2.cloned.1.call-update) | async-done | bytes 1048592 | tf_op jit(solution)/shard_map/all_gather | solution.py:12
  39.2 0.0 copy-done
  39.2 0.0 copy-start.1
  39.2 3.2 %convolution_convert_fusion.1 = bf16[1024,1024]{1,0:T(8,128)(2,1)} fusion(bf16[1024,256]{1,0:T(8,128)(2,1)S(1)} %copy-done, bf16[2,1024,256]{2,1,0:T(8,128)(2,1)} %all-gather.2.cloned.1.call-done), kind=kOutput, calls=%fused_computation.19 | convolution fusion | flops 537919488 | bytes 3145728 | tf_op jit(solution)/shard_map/dot_general | solution.py:100
  42.4 0.0 copy-done.1
  42.4 4.4 %convolution_convert_fusion = bf16[1024,3072]{1,0:T(8,128)(2,1)} fusion(bf16[256,3072]{0,1:T(8,128)(2,1)S(1)} %bitcast.61, bf16[2,1024,256]{2,1,0:T(8,128)(2,1)S(1)} %copy-done.1), kind=kOutput, calls=%fused_computation | convolution fusion | flops 1613758464 | bytes 8388608 | tf_op jit(solution)/shard_map/dot_general | solution.py:99
  46.9 0.0 all-reduce.3.cloned.1.call-update
  47.0 211.8 %all-reduce.3.cloned.1.call-done = (bf16[1024,3072]{1,0:T(8,128)(2,1)}, bf16[1024,1024]{1,0:T(8,128)(2,1)}) async-done(((bf16[1024,3072]{1,0:T(8,128)(2,1)}, bf16[1024,1024]{1,0:T(8,128)(2,1)}), (bf16[1024,3072]{1,0:T(8,128)(2,1)}, bf16[1024,1024]{1,0:T(8,128)(2,1)})) %all-reduce.3.cloned.1.call-update) | async-done | bytes 8388624 | tf_op jit(solution)/shard_map/psum | solution.py:29
  258.8 13.9 %shard_map.92 = (bf16[1024,1024]{1,0:T(8,128)(2,1)}, bf16[1024,1024]{1,0:T(8,128)(2,1)}, bf16[1024,1024]{1,0:T(8,128)(2,1)}, bf16[1024,1024]{1,0:T(8,128)(2,1)}, f32[8,1024]{1,0:T(8,128)}) custom-call(bf16[1024,3072]{1,0:T(8,128)(2,1)} %get-tuple-element.25.q_ref.k_ref.v_ref, bf16[1024,3072]{1,0:T(8,128)(2,1)} %get-tuple-element.25.q_ref.k_ref.v_ref, ...), custom_call_target="tpu_custom_call" | custom-call | flops 62914560 | bytes 18874368 | tf_op jit(solution)/shard_map/pallas_call | solution.py:71
  272.7 0.0 copy-start.8
  272.7 2.4 convolution_convert_fusion.3
  275.2 0.0 copy-start.2
  275.2 0.0 copy-done.8
  275.2 0.0 copy-start.7
  275.2 0.2 constant_dynamic-update-slice_fusion.2
  275.4 1.6 copy-done.7
  277.0 0.0 copy-start.6
  277.0 0.2 constant_dynamic-update-slice_fusion.1
  277.2 1.4 copy-done.6
  278.6 0.2 constant_dynamic-update-slice_fusion
  278.7 1.8 fusion.2
  280.5 0.0 copy-start.4
  280.6 2.0 collective-permute-start.6
  282.6 0.0 copy-done.2
  282.6 0.8 fusion.26
  283.4 0.0 collective-permute-start
  283.5 0.0 collective-permute-start.1
  283.5 1.7 collective-permute-start.2
  285.2 0.0 copy-done.4
  285.2 0.0 copy-start.11
  285.2 2.7 collective-permute-start.3
  287.9 1.9 fusion
  289.8 0.0 collective-permute-done.6
  289.8 1.3 collective-permute-start.4
  291.1 0.0 collective-permute-done
  291.1 1.4 collective-permute-start.5
  292.5 0.0 copy-done.11
  292.5 1.6 fusion.1
  294.1 1.6 copy.13
  295.7 0.0 copy-start.3
  295.7 0.0 copy-start.5
  295.7 0.0 copy-start.9
  295.7 0.0 copy-start.10
  295.7 2.7 copy.14
  298.4 1.4 fusion.29
  299.8 0.0 collective-permute-done.1
  299.8 0.0 collective-permute-done.2
  299.8 0.0 collective-permute-done.3
  299.8 0.0 collective-permute-done.4
  299.8 0.0 collective-permute-done.5
  299.8 0.0 copy-done.3
  299.8 0.0 copy-done.5
  299.8 1.2 fusion.8
  301.0 0.0 copy-done.9
  301.1 0.0 copy-done.10
  301.1 0.7 fusion.18
  (1 shorter events, 0.0 us)
Async XLA Ops:
  7.2 32.0 %copy-start = (bf16[1024,256]{1,0:T(8,128)(2,1)S(1)}, bf16[1024,256]{1,0:T(8,128)(2,1)}, u32[]{:S(2)}) copy-start(bf16[1024,256]{1,0:T(8,128)(2,1)} %param.8) | copy-start | bytes 1572868
  7.2 32.0 %all-gather.2.cloned.1.call-start = ((), (), s32[]{:S(2)}) async-start(), calls=%async_computation | async-start | bytes 1179648 | tf_op jit(solution)/shard_map/all_gather | solution.py:12
  8.8 249.9 %all-reduce.3.cloned.1.call-start = ((), (), s32[]{:S(2)}) async-start(), calls=%async_computation.1 | async-start | bytes 16777216 | tf_op jit(solution)/shard_map/psum | solution.py:29
  39.2 3.2 %copy-start.1 = (bf16[2,1024,256]{2,1,0:T(8,128)(2,1)S(1)}, bf16[2,1024,256]{2,1,0:T(8,128)(2,1)}, u32[]{:S(2)}) copy-start(bf16[2,1024,256]{2,1,0:T(8,128)(2,1)} %all-gather.2.cloned.1.call-done) | copy-start | bytes 3145732
  272.7 2.5 copy-start.8
  275.2 7.4 %copy-start.2 = (bf16[1024,256]{1,0:T(8,128)(2,1)}, bf16[1024,256]{1,0:T(8,128)(2,1)S(1)}, u32[]{:S(2)}) copy-start(bf16[1024,256]{1,0:T(8,128)(2,1)S(1)} %convolution_convert_fusion.3) | copy-start | bytes 1572868
  275.2 1.8 copy-start.7
  277.0 1.6 copy-start.6
  280.5 4.6 %copy-start.4 = (bf16[1,8,128,256]{3,2,1,0:T(8,128)(2,1)}, bf16[1,8,128,256]{3,2,1,0:T(8,128)(2,1)S(1)}, u32[]{:S(2)}) copy-start(bf16[1,8,128,256]{3,2,1,0:T(8,128)(2,1)S(1)} %fusion.2) | copy-start | bytes 1572868
  280.6 9.2 %collective-permute-start.6 = (bf16[2,128,256]{2,1,0:T(8,128)(2,1)S(1)}, bf16[2,128,256]{2,1,0:T(8,128)(2,1)S(1)}, u32[]{:S(2)}, u32[]{:S(2)}) collective-permute-start(bf16[2,128,256]{2,1,0:T(8,128)(2,1)S(1)} %fusion.27), channel_id=1, source_target_pairs={{0,224},{32,0},{64,32},{96,64},{128,96},{160,128},{192,160},{224,1... | collective-permute-start | bytes 393224 | tf_op jit(solution)/shard_map/ppermute | solution.py:24
  283.4 7.7 %collective-permute-start = (bf16[2,128,256]{2,1,0:T(8,128)(2,1)S(1)}, bf16[2,128,256]{2,1,0:T(8,128)(2,1)S(1)}, u32[]{:S(2)}, u32[]{:S(2)}) collective-permute-start(bf16[2,128,256]{2,1,0:T(8,128)(2,1)S(1)} %get-tuple-element.27), channel_id=1, source_target_pairs={{0,32},{32,64},{64,96},{96,128},{128,160},{160,192},{192,224},{224... | collective-permute-start | bytes 393224 | tf_op jit(solution)/shard_map/ppermute | solution.py:24
  283.5 16.3 %collective-permute-start.1 = (bf16[2,128,256]{2,1,0:T(8,128)(2,1)}, bf16[2,128,256]{2,1,0:T(8,128)(2,1)S(1)}, u32[]{:S(2)}, u32[]{:S(2)}) collective-permute-start(bf16[2,128,256]{2,1,0:T(8,128)(2,1)} %get-tuple-element.28), channel_id=1, source_target_pairs={{0,64},{32,96},{64,128},{96,160},{128,192},{160,224},{192,0},{224,... | collective-permute-start | bytes 393224 | tf_op jit(solution)/shard_map/ppermute | solution.py:24
  283.5 16.3 %collective-permute-start.2 = (bf16[2,128,256]{2,1,0:T(8,128)(2,1)}, bf16[2,128,256]{2,1,0:T(8,128)(2,1)}, u32[]{:S(2)}, u32[]{:S(2)}) collective-permute-start(bf16[2,128,256]{2,1,0:T(8,128)(2,1)} %get-tuple-element.29), channel_id=1, source_target_pairs={{0,96},{32,128},{64,160},{96,192},{128,224},{160,0},{192,32},{224,... | collective-permute-start | bytes 393224 | tf_op jit(solution)/shard_map/ppermute | solution.py:24
  285.2 7.4 %copy-start.11 = (bf16[1024,1024]{1,0:T(8,128)(2,1)S(1)}, bf16[1024,1024]{1,0:T(8,128)(2,1)}, u32[]{:S(2)}) copy-start(bf16[1024,1024]{1,0:T(8,128)(2,1)} %get-tuple-element.10) | copy-start | bytes 6291460
  285.2 14.6 %collective-permute-start.3 = (bf16[2,128,256]{2,1,0:T(8,128)(2,1)}, bf16[2,128,256]{2,1,0:T(8,128)(2,1)}, u32[]{:S(2)}, u32[]{:S(2)}) collective-permute-start(bf16[2,128,256]{2,1,0:T(8,128)(2,1)} %get-tuple-element.30), channel_id=1, source_target_pairs={{0,128},{32,160},{64,192},{96,224},{128,0},{160,32},{192,64},{224,... | collective-permute-start | bytes 393224 | tf_op jit(solution)/shard_map/ppermute | solution.py:24
  289.8 10.0 %collective-permute-start.4 = (bf16[2,128,256]{2,1,0:T(8,128)(2,1)}, bf16[2,128,256]{2,1,0:T(8,128)(2,1)}, u32[]{:S(2)}, u32[]{:S(2)}) collective-permute-start(bf16[2,128,256]{2,1,0:T(8,128)(2,1)} %get-tuple-element.31), channel_id=1, source_target_pairs={{0,160},{32,192},{64,224},{96,0},{128,32},{160,64},{192,96},{224,1... | collective-permute-start | bytes 393224 | tf_op jit(solution)/shard_map/ppermute | solution.py:24
  291.1 8.7 %collective-permute-start.5 = (bf16[2,128,256]{2,1,0:T(8,128)(2,1)}, bf16[2,128,256]{2,1,0:T(8,128)(2,1)}, u32[]{:S(2)}, u32[]{:S(2)}) collective-permute-start(bf16[2,128,256]{2,1,0:T(8,128)(2,1)} %get-tuple-element.32), channel_id=1, source_target_pairs={{0,192},{32,224},{64,0},{96,32},{128,64},{160,96},{192,128},{224,1... | collective-permute-start | bytes 393224 | tf_op jit(solution)/shard_map/ppermute | solution.py:24
  295.7 4.1 %copy-start.3 = (bf16[1024,256]{1,0:T(8,128)(2,1)S(1)}, bf16[1024,256]{1,0:T(8,128)(2,1)}, u32[]{:S(2)}) copy-start(bf16[1024,256]{1,0:T(8,128)(2,1)} %copy-done.2) | copy-start | bytes 1572868
  295.7 4.1 %copy-start.5 = (bf16[1,8,128,256]{3,2,1,0:T(8,128)(2,1)S(1)}, bf16[1,8,128,256]{3,2,1,0:T(8,128)(2,1)}, u32[]{:S(2)}) copy-start(bf16[1,8,128,256]{3,2,1,0:T(8,128)(2,1)} %copy-done.4) | copy-start | bytes 1572868
  295.7 5.3 %copy-start.9 = (bf16[128,256]{1,0:T(8,128)(2,1)S(1)}, bf16[128,256]{1,0:T(8,128)(2,1)}, u32[]{:S(2)}) copy-start(bf16[128,256]{1,0:T(8,128)(2,1)} %param.6) | copy-start | bytes 196612
  295.7 5.3 %copy-start.10 = (bf16[128,256]{1,0:T(8,128)(2,1)S(1)}, bf16[128,256]{1,0:T(8,128)(2,1)}, u32[]{:S(2)}) copy-start(bf16[128,256]{1,0:T(8,128)(2,1)} %param.5) | copy-start | bytes 196612
Sparse Core Ops, SparseCore 0:
  10.4 28.7 all-gather.1
  47.0 211.7 all-reduce.2
